TPU v7x, 512 devices: a whole 4x4x16 slice. The times are simulated.
512 devices in a mesh: req: 64 (over z, x), head: 8 (over y, core).
Axes of the slice: x: 4, y: 4, z: 16, core: 2. Of those that a mesh axis runs over, the one named last changes fastest.
Arguments:
- tokens: bfloat16 [128, 1024], P('req'), may hold values from -6 to 6
- self_keys: bfloat16 [128, 512, 1024], P('req', None, 'head'), may hold values from -240 to 240
- self_values: bfloat16 [128, 512, 1024], P('req', None, 'head'), may hold values from -6 to 6
- self_len: int32 [128], P('req'), may hold values from 1 to 512, as said below
- cross_keys: bfloat16 [128, 512, 1024], P('req', None, 'head'), may hold values from -240 to 240
- cross_values: bfloat16 [128, 512, 1024], P('req', None, 'head'), may hold values from -6 to 6
- cross_len: int32 [128], P('req'), may hold values from 1 to 512, as said below
- give_slot: int32 [64], P('req'), may hold values from 0 to 1
- w_query: bfloat16 [1024, 1024], P(None, 'head'), may hold values from -0.1875 to 0.1875
- w_key: bfloat16 [1024, 1024], P(None, 'head'), may hold values from -0.1875 to 0.1875
- w_value: bfloat16 [1024, 1024], P(None, 'head'), may hold values from -0.1875 to 0.1875
- w_out: bfloat16 [1024, 1024], P('head'), may hold values from -0.1875 to 0.1875
- w_cross_query: bfloat16 [1024, 1024], P(None, 'head'), may hold values from -0.1875 to 0.1875
- w_cross_out: bfloat16 [1024, 1024], P('head'), may hold values from -0.1875 to 0.1875
- w_up: bfloat16 [1024, 4096], P(None, 'head'), may hold values from -0.1875 to 0.1875
- w_down: bfloat16 [4096, 1024], P('head'), may hold values from -0.09375 to 0.09375
- gain_self: float32 [1024], replicated, may hold values from 0.1 to 1.9
- gain_cross: float32 [1024], replicated, may hold values from 0.1 to 1.9
- gain_final: float32 [1024], replicated, may hold values from 0.1 to 1.9
Outputs:
- decoded: bfloat16 [128, 1024], P('req')
- new_keys: bfloat16 [128, 1024], P('req', 'head')
- new_values: bfloat16 [128, 1024], P('req', 'head')
- moved_keys: bfloat16 [64, 512, 1024], P('req', None, 'head')
- moved_values: bfloat16 [64, 512, 1024], P('req', None, 'head')
Inputs may be any that keep to these rules, and one draw needn't show every extreme that they name: `self_len`: each request fills at least one slot; some request fills all 512. `cross_len`: each request has at least one encoder position; some request has 512.
All inputs are finite; a program needn't handle non-finite values.
Results may differ from a plain program's by a relative error of at most 0.039.
Values may be sent and summed in bfloat16 or wider, within the bound.
No kernel may reach another device: no remote copies, remote signals or barrier semaphores. Data moves between devices by JAX's collectives and lax.ppermute only.
A program may use at most 64 MiB of HBM per device.

v0:
```python
import jax
import jax.numpy as jnp
from jax import lax
from jax.sharding import PartitionSpec as P

HEAD_DIM = 64


def passed_along(block, axis, distance):
    devices = range(lax.axis_size(axis))
    route = [((i - distance) % len(devices), i) for i in devices]
    return lax.ppermute(block, axis, route)


def layer_norm(value, gain):
    mean = jnp.mean(value, axis=-1, keepdims=True)
    centred = value - mean
    spread = jnp.mean(centred * centred, axis=-1, keepdims=True)
    return centred * lax.rsqrt(spread + 1e-05) * gain


def attend(query, keys, values, lengths, fresh_key, fresh_value):
    count, span, width = keys.shape
    heads = width // HEAD_DIM
    block = min(512, span)
    query_heads = query.reshape(count, heads, HEAD_DIM)
    steps = (jnp.max(lengths) + block - 1) // block
    places = lax.iota(jnp.int32, block)

    def score_block(index, board):
        start = index * block
        piece = keys.reshape(count, block, heads, HEAD_DIM)
        scores = jnp.einsum("qhd,qshd->qhs", query_heads, piece, preferred_element_type=jnp.float32)
        valid = (start + places)[None, None, :] < lengths[:, None, None]
        scores = jnp.where(valid, scores, -jnp.inf)
        return scores

    board = lax.fori_loop(
        0, steps, score_block, jnp.full((count, heads, span), -jnp.inf, jnp.float32)
    )
    top = jnp.max(board, axis=2)
    if fresh_key is not None:
        own = jnp.sum(
            query_heads.astype(jnp.float32)
            * fresh_key.reshape(count, heads, HEAD_DIM).astype(jnp.float32),
            axis=2,
        )
        top = jnp.maximum(top, own)
    weights_all = jnp.exp(board - top[:, :, None])
    total = jnp.sum(weights_all, axis=2)

    def mix_block(index, accum):
        start = index * block
        weights = weights_all.astype(jnp.bfloat16)
        piece = values.reshape(count, block, heads, HEAD_DIM)
        return accum + jnp.einsum(
            "qhs,qshd->qhd", weights, piece, preferred_element_type=jnp.float32
        )

    mixed = lax.fori_loop(0, steps, mix_block, jnp.zeros((count, heads, HEAD_DIM), jnp.float32))
    if fresh_key is not None:
        own_weight = jnp.exp(own - top)
        total = total + own_weight
        mixed = mixed + own_weight.astype(jnp.bfloat16).astype(jnp.float32)[
            :, :, None
        ] * fresh_value.reshape(count, heads, HEAD_DIM).astype(jnp.float32)
    return (mixed / total[:, :, None]).astype(jnp.bfloat16).reshape(count, width)


def decode_layer(
    tokens, self_keys, self_values, self_len, cross_keys, cross_values, cross_len, params
):
    (
        w_query,
        w_key,
        w_value,
        w_out,
        w_cross_query,
        w_cross_out,
        w_up,
        w_down,
        gain_self,
        gain_cross,
        gain_final,
    ) = params
    scale = HEAD_DIM ** (-0.5)
    query = (jnp.dot(tokens, w_query, preferred_element_type=jnp.float32) * scale).astype(
        jnp.bfloat16
    )
    fresh_keys = jnp.dot(tokens, w_key, preferred_element_type=jnp.float32).astype(jnp.bfloat16)
    fresh_values = jnp.dot(tokens, w_value, preferred_element_type=jnp.float32).astype(jnp.bfloat16)
    self_mixed = attend(query, self_keys, self_values, self_len, fresh_keys, fresh_values)
    self_total = lax.psum(jnp.dot(self_mixed, w_out, preferred_element_type=jnp.float32), "head")
    first = layer_norm(tokens.astype(jnp.float32) + self_total, gain_self).astype(jnp.bfloat16)
    cross_query = (
        jnp.dot(first, w_cross_query, preferred_element_type=jnp.float32) * scale
    ).astype(jnp.bfloat16)
    cross_mixed = attend(cross_query, cross_keys, cross_values, cross_len, None, None)
    cross_total = lax.psum(
        jnp.dot(cross_mixed, w_cross_out, preferred_element_type=jnp.float32), "head"
    )
    second = layer_norm(first.astype(jnp.float32) + cross_total, gain_cross).astype(jnp.bfloat16)
    hidden = jax.nn.gelu(
        jnp.dot(second, w_up, preferred_element_type=jnp.float32), approximate=False
    ).astype(jnp.bfloat16)
    ffn_total = lax.psum(jnp.dot(hidden, w_down, preferred_element_type=jnp.float32), "head")
    layer_out = layer_norm(second.astype(jnp.float32) + ffn_total, gain_final).astype(jnp.bfloat16)
    return (layer_out, fresh_keys, fresh_values)


def take_slot(array, chosen):
    return lax.dynamic_slice_in_dim(array, chosen, 1, 0)


def put_slot(array, row, chosen):
    return lax.dynamic_update_slice_in_dim(array, row, chosen, 0)


def on_device(
    tokens,
    self_keys,
    self_values,
    self_len,
    cross_keys,
    cross_values,
    cross_len,
    give_slot,
    w_query,
    w_key,
    w_value,
    w_out,
    w_cross_query,
    w_cross_out,
    w_up,
    w_down,
    gain_self,
    gain_cross,
    gain_final,
):
    params = (
        w_query,
        w_key,
        w_value,
        w_out,
        w_cross_query,
        w_cross_out,
        w_up,
        w_down,
        gain_self,
        gain_cross,
        gain_final,
    )
    chosen = give_slot[0]
    half_axis = lax.axis_size("req") // 2
    moving = passed_along(
        (
            take_slot(tokens, chosen),
            take_slot(self_keys, chosen),
            take_slot(self_values, chosen),
            take_slot(cross_keys, chosen),
            take_slot(cross_values, chosen),
        ),
        "req",
        half_axis,
    )
    arrived_len = passed_along(
        (take_slot(self_len, chosen), take_slot(cross_len, chosen)), "req", half_axis
    )
    decoded, new_keys, new_values = decode_layer(
        put_slot(tokens, moving[0], chosen),
        put_slot(self_keys, moving[1], chosen),
        put_slot(self_values, moving[2], chosen),
        put_slot(self_len, arrived_len[0], chosen),
        put_slot(cross_keys, moving[3], chosen),
        put_slot(cross_values, moving[4], chosen),
        put_slot(cross_len, arrived_len[1], chosen),
        params,
    )
    moved_keys = moving[1]
    moved_values = moving[2]
    return (decoded, new_keys, new_values, moved_keys, moved_values)


def solution(mesh):
    placed = (
        P("req", None),
        P("req", None, "head"),
        P("req", None, "head"),
        P("req"),
        P("req", None, "head"),
        P("req", None, "head"),
        P("req"),
        P("req"),
        P(None, "head"),
        P(None, "head"),
        P(None, "head"),
        P("head", None),
        P(None, "head"),
        P("head", None),
        P(None, "head"),
        P("head", None),
        P(),
        P(),
        P(),
    )
    return jax.shard_map(
        on_device,
        mesh=mesh,
        in_specs=placed,
        out_specs=(
            P("req", None),
            P("req", "head"),
            P("req", "head"),
            P("req", None, "head"),
            P("req", None, "head"),
        ),
        check_vma=False,
    )
```

profile of v0, /device:TPU:1, one launch (start us, length us, event | category | flops | bytes accessed | tf_op | source)
XLA Modules:
  0.0 135.8 jit_solution(12069132178219028557)
XLA Ops:
  0.6 0.7 copy.88
  1.4 0.7 copy.87
  3.3 16.2 %collective-permute-start.1 = (s32[1]{0:T(128)}, s32[1]{0:T(128)}, u32[]{:S(2)}, u32[]{:S(2)}) collective-permute-start(s32[1]{0:T(128)} %dynamic_slice.22), channel_id=1, source_target_pairs={{256,0},{264,8},{272,16},{280,24},{288,32},{296,40},{304,48},{312,... | collective-permute-start | bytes 20 | tf_op jit(solution)/shard_map/ppermute | solution.py:12
  19.6 1.9 %collective-permute-start = (bf16[1,1024]{1,0:T(2,128)(2,1)S(1)}, bf16[1,1024]{1,0:T(2,128)(2,1)S(1)}, u32[]{:S(2)}, u32[]{:S(2)}) collective-permute-start(bf16[1,1024]{1,0:T(2,128)(2,1)S(1)} %constant_dynamic-slice_fusion.4), channel_id=1, source_target_pairs={{256,0},{264,8},{272,16},{280,24},{288,32},{296,40},{304,48},{312,... | collective-permute-start | bytes 6152 | tf_op jit(solution)/shard_map/ppermute | solution.py:12
  21.6 1.1 copy.25
  22.7 0.7 constant_dynamic-slice_fusion.3
  23.3 12.1 %collective-permute-start.2 = (bf16[1,512,128]{1,2,0:T(8,128)(2,1)}, bf16[1,512,128]{1,2,0:T(8,128)(2,1)S(1)}, u32[]{:S(2)}, u32[]{:S(2)}) collective-permute-start(bf16[1,512,128]{1,2,0:T(8,128)(2,1)} %constant_dynamic-slice_fusion.3), channel_id=1, source_target_pairs={{256,0},{264,8},{272,16},{280,24},{288,32},{296,40},{304,48},{312,... | collective-permute-start | bytes 393224 | tf_op jit(solution)/shard_map/ppermute | solution.py:12
  35.6 2.1 %collective-permute-start.3 = (bf16[1,512,128]{1,2,0:T(8,128)(2,1)S(1)}, bf16[1,512,128]{1,2,0:T(8,128)(2,1)S(1)}, u32[]{:S(2)}, u32[]{:S(2)}) collective-permute-start(bf16[1,512,128]{1,2,0:T(8,128)(2,1)S(1)} %constant_dynamic-slice_fusion.2), channel_id=1, source_target_pairs={{256,0},{264,8},{272,16},{280,24},{288,32},{296,40},{304,48},{312,... | collective-permute-start | bytes 393224 | tf_op jit(solution)/shard_map/ppermute | solution.py:12
  37.8 0.7 constant_dynamic-slice_fusion.1
  38.5 12.1 %collective-permute-start.5 = (bf16[1,512,128]{1,2,0:T(8,128)(2,1)}, bf16[1,512,128]{1,2,0:T(8,128)(2,1)S(1)}, u32[]{:S(2)}, u32[]{:S(2)}) collective-permute-start(bf16[1,512,128]{1,2,0:T(8,128)(2,1)} %constant_dynamic-slice_fusion.1), channel_id=1, source_target_pairs={{256,0},{264,8},{272,16},{280,24},{288,32},{296,40},{304,48},{312,... | collective-permute-start | bytes 393224 | tf_op jit(solution)/shard_map/ppermute | solution.py:12
  51.4 2.1 %collective-permute-start.4 = (s32[1]{0:T(128)}, s32[1]{0:T(128)}, u32[]{:S(2)}, u32[]{:S(2)}) collective-permute-start(s32[1]{0:T(128)} %dynamic_slice.25), channel_id=1, source_target_pairs={{256,0},{264,8},{272,16},{280,24},{288,32},{296,40},{304,48},{312,... | collective-permute-start | bytes 20 | tf_op jit(solution)/shard_map/ppermute | solution.py:12
  53.4 0.8 dynamic_update_slice.22
  54.2 0.6 reduce_max.36
  55.5 16.9 %collective-permute-done.4 = s32[1]{0:T(128)} collective-permute-done((s32[1]{0:T(128)}, s32[1]{0:T(128)}, u32[]{:S(2)}, u32[]{:S(2)}) %collective-permute-start.4) | collective-permute-done | bytes 36 | tf_op jit(solution)/shard_map/ppermute | solution.py:12
  72.4 4.9 %collective-permute-start.6 = (bf16[1,512,128]{1,2,0:T(8,128)(2,1)S(1)}, bf16[1,512,128]{1,2,0:T(8,128)(2,1)S(1)}, u32[]{:S(2)}, u32[]{:S(2)}) collective-permute-start(bf16[1,512,128]{1,2,0:T(8,128)(2,1)S(1)} %constant_dynamic-slice_fusion), channel_id=1, source_target_pairs={{256,0},{264,8},{272,16},{280,24},{288,32},{296,40},{304,48},{312,... | collective-permute-start | bytes 393224 | tf_op jit(solution)/shard_map/ppermute | solution.py:12
  77.3 0.7 dynamic_update_slice.25
  78.1 0.6 reduce_max.38
  79.8 0.6 copy-done.7
  81.5 0.6 broadcast.133.clone
  82.1 0.7 while.52
  82.1 0.6 broadcast_select_fusion.4
  82.8 0.9 reduce_max.37
  84.9 16.8 %psum.21 = f32[2,1024]{1,0:T(2,128)S(1)} all-reduce(f32[2,1024]{1,0:T(2,128)S(1)} %fusion.92), channel_id=1, replica_groups=mesh['req'=64,'head'=8] {'head'}, use_global_device_ids=true, to_apply=%region_8.9 | all-reduce | flops 2048 | bytes 16384 | tf_op jit(solution)/shard_map/psum | solution.py:93
  102.6 0.6 broadcast.133
  103.2 0.7 while.53
  103.3 0.6 broadcast_select_fusion.5
  103.9 0.9 fusion.6
  106.0 13.7 %psum.22 = f32[2,1024]{1,0:T(2,128)S(1)} all-reduce(f32[2,1024]{1,0:T(2,128)S(1)} %fusion.94), channel_id=1, replica_groups=mesh['req'=64,'head'=8] {'head'}, use_global_device_ids=true, to_apply=%region_18.19 | all-reduce | flops 2048 | bytes 16384 | tf_op jit(solution)/shard_map/psum | solution.py:99
  120.6 12.6 %psum.23 = f32[2,1024]{1,0:T(2,128)S(1)} all-reduce(f32[2,1024]{1,0:T(2,128)S(1)} %fusion.21), channel_id=1, replica_groups=mesh['req'=64,'head'=8] {'head'}, use_global_device_ids=true, to_apply=%region_21.22 | all-reduce | flops 2048 | bytes 16384 | tf_op jit(solution)/shard_map/psum | solution.py:106
  133.6 0.7 multiply_convert_fusion
  134.3 0.8 copy.32
  135.0 0.8 copy.33
  (106 shorter events, 7.8 us)
Async XLA Ops:
  0.6 119.4 %copy-start = (bf16[512,1024]{1,0:T(8,128)(2,1)S(1)}, bf16[512,1024]{1,0:T(8,128)(2,1)}, u32[]{:S(2)}) copy-start(bf16[512,1024]{1,0:T(8,128)(2,1)} %param.42) | copy-start | bytes 3145732
  1.4 0.7 copy-start.17
  3.3 48.0 %collective-permute-start.1 = (s32[1]{0:T(128)}, s32[1]{0:T(128)}, u32[]{:S(2)}, u32[]{:S(2)}) collective-permute-start(s32[1]{0:T(128)} %dynamic_slice.22), channel_id=1, source_target_pairs={{256,0},{264,8},{272,16},{280,24},{288,32},{296,40},{304,48},{312,... | collective-permute-start | bytes 20 | tf_op jit(solution)/shard_map/ppermute | solution.py:12
  19.6 59.8 %collective-permute-start = (bf16[1,1024]{1,0:T(2,128)(2,1)S(1)}, bf16[1,1024]{1,0:T(2,128)(2,1)S(1)}, u32[]{:S(2)}, u32[]{:S(2)}) collective-permute-start(bf16[1,1024]{1,0:T(2,128)(2,1)S(1)} %constant_dynamic-slice_fusion.4), channel_id=1, source_target_pairs={{256,0},{264,8},{272,16},{280,24},{288,32},{296,40},{304,48},{312,... | collective-permute-start | bytes 6152 | tf_op jit(solution)/shard_map/ppermute | solution.py:12
  22.6 12.8 %copy-start.2 = (bf16[2,512,128]{2,1,0:T(8,128)(2,1)S(1)}, bf16[2,512,128]{2,1,0:T(8,128)(2,1)}, u32[]{:S(2)}) copy-start(bf16[2,512,128]{2,1,0:T(8,128)(2,1)} %param.29) | copy-start | bytes 786436
  23.3 58.0 %collective-permute-start.2 = (bf16[1,512,128]{1,2,0:T(8,128)(2,1)}, bf16[1,512,128]{1,2,0:T(8,128)(2,1)S(1)}, u32[]{:S(2)}, u32[]{:S(2)}) collective-permute-start(bf16[1,512,128]{1,2,0:T(8,128)(2,1)} %constant_dynamic-slice_fusion.3), channel_id=1, source_target_pairs={{256,0},{264,8},{272,16},{280,24},{288,32},{296,40},{304,48},{312,... | collective-permute-start | bytes 393224 | tf_op jit(solution)/shard_map/ppermute | solution.py:12
  35.6 2.1 %copy-start.3 = (bf16[2,512,128]{2,1,0:T(8,128)(2,1)S(1)}, bf16[2,512,128]{2,1,0:T(8,128)(2,1)}, u32[]{:S(2)}) copy-start(bf16[2,512,128]{2,1,0:T(8,128)(2,1)} %param.31) | copy-start | bytes 786436
  35.6 48.2 %collective-permute-start.3 = (bf16[1,512,128]{1,2,0:T(8,128)(2,1)S(1)}, bf16[1,512,128]{1,2,0:T(8,128)(2,1)S(1)}, u32[]{:S(2)}, u32[]{:S(2)}) collective-permute-start(bf16[1,512,128]{1,2,0:T(8,128)(2,1)S(1)} %constant_dynamic-slice_fusion.2), channel_id=1, source_target_pairs={{256,0},{264,8},{272,16},{280,24},{288,32},{296,40},{304,48},{312,... | collective-permute-start | bytes 393224 | tf_op jit(solution)/shard_map/ppermute | solution.py:12
  37.8 13.3 %copy-start.4 = (bf16[2,512,128]{2,1,0:T(8,128)(2,1)S(1)}, bf16[2,512,128]{2,1,0:T(8,128)(2,1)}, u32[]{:S(2)}) copy-start(bf16[2,512,128]{2,1,0:T(8,128)(2,1)} %param.32) | copy-start | bytes 786436
  38.5 63.9 %collective-permute-start.5 = (bf16[1,512,128]{1,2,0:T(8,128)(2,1)}, bf16[1,512,128]{1,2,0:T(8,128)(2,1)S(1)}, u32[]{:S(2)}, u32[]{:S(2)}) collective-permute-start(bf16[1,512,128]{1,2,0:T(8,128)(2,1)} %constant_dynamic-slice_fusion.1), channel_id=1, source_target_pairs={{256,0},{264,8},{272,16},{280,24},{288,32},{296,40},{304,48},{312,... | collective-permute-start | bytes 393224 | tf_op jit(solution)/shard_map/ppermute | solution.py:12
  51.3 28.2 %copy-start.5 = (bf16[1024,128]{1,0:T(8,128)(2,1)S(1)}, bf16[1024,128]{1,0:T(8,128)(2,1)}, u32[]{:S(2)}) copy-start(bf16[1024,128]{1,0:T(8,128)(2,1)} %param.35) | copy-start | bytes 786436
  51.3 28.3 %copy-start.6 = (bf16[1024,128]{1,0:T(8,128)(2,1)S(1)}, bf16[1024,128]{1,0:T(8,128)(2,1)}, u32[]{:S(2)}) copy-start(bf16[1024,128]{1,0:T(8,128)(2,1)} %param.36) | copy-start | bytes 786436
  51.4 21.0 %collective-permute-start.4 = (s32[1]{0:T(128)}, s32[1]{0:T(128)}, u32[]{:S(2)}, u32[]{:S(2)}) collective-permute-start(s32[1]{0:T(128)} %dynamic_slice.25), channel_id=1, source_target_pairs={{256,0},{264,8},{272,16},{280,24},{288,32},{296,40},{304,48},{312,... | collective-permute-start | bytes 20 | tf_op jit(solution)/shard_map/ppermute | solution.py:12
  72.4 32.4 %collective-permute-start.6 = (bf16[1,512,128]{1,2,0:T(8,128)(2,1)S(1)}, bf16[1,512,128]{1,2,0:T(8,128)(2,1)S(1)}, u32[]{:S(2)}, u32[]{:S(2)}) collective-permute-start(bf16[1,512,128]{1,2,0:T(8,128)(2,1)S(1)} %constant_dynamic-slice_fusion), channel_id=1, source_target_pairs={{256,0},{264,8},{272,16},{280,24},{288,32},{296,40},{304,48},{312,... | collective-permute-start | bytes 393224 | tf_op jit(solution)/shard_map/ppermute | solution.py:12
  79.5 1.0 copy-start.7
  80.4 0.5 copy-start.15
  80.6 0.5 copy-start.16
  82.8 0.9 copy-start.11
  83.8 1.0 copy-start.8
  84.0 18.1 %copy-start.9 = (bf16[1024,128]{1,0:T(8,128)(2,1)S(1)}, bf16[1024,128]{1,0:T(8,128)(2,1)}, u32[]{:S(2)}) copy-start(bf16[1024,128]{1,0:T(8,128)(2,1)} %param.39) | copy-start | bytes 786436
  84.8 17.3 %copy-start.12 = (f32[1024]{0:T(1024)S(1)}, f32[1024]{0:T(1024)}, u32[]{:S(2)}) copy-start(f32[1024]{0:T(1024)} %param.43) | copy-start | bytes 12292
  102.1 17.9 %copy-start.1 = (bf16[1024,512]{1,0:T(8,128)(2,1)S(1)}, bf16[1024,512]{1,0:T(8,128)(2,1)}, u32[]{:S(2)}) copy-start(bf16[1024,512]{1,0:T(8,128)(2,1)} %param.41) | copy-start | bytes 3145732
  104.8 1.0 copy-start.10
  105.8 14.2 %copy-start.13 = (f32[1024]{0:T(1024)S(1)}, f32[1024]{0:T(1024)}, u32[]{:S(2)}) copy-start(f32[1024]{0:T(1024)} %param.44) | copy-start | bytes 12292
  120.1 13.5 %copy-start.14 = (f32[1024]{0:T(1024)S(1)}, f32[1024]{0:T(1024)}, u32[]{:S(2)}) copy-start(f32[1024]{0:T(1024)} %param.45) | copy-start | bytes 12292
where the time goes:
time: 136 us
  starting transfers between devices  51.3 us (38%)
  blocking collectives  43.1 us (32%)
  waiting for transfers between devices  16.9 us (12%)
  local copies, waits for them, and re-layouts  12.7 us (9%)
  other arithmetic  6.73 us (5%)
  between operations  3.02 us (2%)
  matrix products  2 us (1%)
    ppermute x7, starting transfers between devices, passed_along(): return lax.ppermute(block, axis, route)  51.3 us
    ppermute x7, waiting for transfers between devices, passed_along(): return lax.ppermute(block, axis, route)  16.9 us
    psum x1, blocking collectives, decode_layer(): lax.psum(jnp.dot(self_mixed, w_out, preferred_element_type=jnp.float32),...  16.8 us
    psum x1, blocking collectives, decode_layer(): lax.psum(jnp.dot(cross_mixed, w_cross_out, preferred_element_type=jnp.flo...  13.7 us
    psum x1, blocking collectives, decode_layer(): lax.psum(jnp.dot(hidden, w_down, preferred_element_type=jnp.float32), 'he...  12.6 us
    unnamed x45, local copies, waits for them, and re-layouts  6.63 us
  transfers between devices with their start and end apart: 7, of which 1 were waited for; matrix products, arithmetic and copies ran while one was open for 10% of the time, Pallas kernels for 0%

commit v1 on v0

--- a/solution.py
+++ b/solution.py
@@ -50,7 +50,6 @@
     total = jnp.sum(weights_all, axis=2)
 
     def mix_block(index, accum):
-        start = index * block
         weights = weights_all.astype(jnp.bfloat16)
         piece = values.reshape(count, block, heads, HEAD_DIM)
         return accum + jnp.einsum(
@@ -152,32 +151,24 @@
     )
     chosen = give_slot[0]
     half_axis = lax.axis_size("req") // 2
-    moving = passed_along(
+    moved_keys, moved_values = passed_along(
+        (take_slot(self_keys, chosen), take_slot(self_values, chosen)), "req", half_axis
+    )
+    layer_out, fresh_keys, fresh_values = decode_layer(
+        tokens, self_keys, self_values, self_len, cross_keys, cross_values, cross_len, params
+    )
+    arrived = passed_along(
         (
-            take_slot(tokens, chosen),
-            take_slot(self_keys, chosen),
-            take_slot(self_values, chosen),
-            take_slot(cross_keys, chosen),
-            take_slot(cross_values, chosen),
+            take_slot(layer_out, chosen),
+            take_slot(fresh_keys, chosen),
+            take_slot(fresh_values, chosen),
         ),
         "req",
         half_axis,
     )
-    arrived_len = passed_along(
-        (take_slot(self_len, chosen), take_slot(cross_len, chosen)), "req", half_axis
-    )
-    decoded, new_keys, new_values = decode_layer(
-        put_slot(tokens, moving[0], chosen),
-        put_slot(self_keys, moving[1], chosen),
-        put_slot(self_values, moving[2], chosen),
-        put_slot(self_len, arrived_len[0], chosen),
-        put_slot(cross_keys, moving[3], chosen),
-        put_slot(cross_values, moving[4], chosen),
-        put_slot(cross_len, arrived_len[1], chosen),
-        params,
-    )
-    moved_keys = moving[1]
-    moved_values = moving[2]
+    decoded = put_slot(layer_out, arrived[0], chosen)
+    new_keys = put_slot(fresh_keys, arrived[1], chosen)
+    new_values = put_slot(fresh_values, arrived[2], chosen)
     return (decoded, new_keys, new_values, moved_keys, moved_values)
 
 

time: 136 us -> 109 us (0.80)
  waiting for transfers between devices: 16.9 us -> 5.09 us
  starting transfers between devices: 51.3 us -> 40.5 us
  local copies, waits for them, and re-layouts: 12.7 us -> 6.84 us
    ppermute x7 -> x5, waiting for transfers between devices: 16.9 us -> 5.09 us  [passed_along(): return lax.ppermute(block, axis, route)]
    ppermute x7 -> x5, starting transfers between devices: 51.3 us -> 40.5 us  [passed_along(): return lax.ppermute(block, axis, route)]
    dynamic_slice x7 -> x5, local copies, waits for them, and re-layouts: 2.57 us -> 0.07 us  [take_slot(): return lax.dynamic_slice_in_dim(array, chosen, 1, 0)]
    psum x1, blocking collectives: 16.8 us -> 18.8 us  [decode_layer(): lax.psum(jnp.dot(self_mixed, w_out, preferred_element_type=jnp.float32),...]
    unnamed x45 -> x48, local copies, waits for them, and re-layouts: 6.63 us -> 4.83 us
    dynamic_update_slice x7 -> x3, local copies, waits for them, and re-layouts: 1.65 us -> 0.11 us  [put_slot(): return lax.dynamic_update_slice_in_dim(array, row, chosen, 0)]
  transfers between devices with their start and end apart: 7 -> 5, of which waited for: 1 -> 1; matrix products, arithmetic and copies ran while one was open for 10% -> 0% of each run, Pallas kernels for 0% -> 0%
where the time goes in v1:
time: 109 us
  blocking collectives  44.1 us (40%)
  starting transfers between devices  40.5 us (37%)
  local copies, waits for them, and re-layouts  6.84 us (6%)
  other arithmetic  6.13 us (6%)
  waiting for transfers between devices  5.09 us (5%)
  matrix products  2.97 us (3%)
  between operations  2.94 us (3%)
    ppermute x5, starting transfers between devices, passed_along(): return lax.ppermute(block, axis, route)  40.5 us
    psum x1, blocking collectives, decode_layer(): lax.psum(jnp.dot(self_mixed, w_out, preferred_element_type=jnp.float32),...  18.8 us
    psum x1, blocking collectives, decode_layer(): lax.psum(jnp.dot(cross_mixed, w_cross_out, preferred_element_type=jnp.flo...  12.6 us
    psum x1, blocking collectives, decode_layer(): lax.psum(jnp.dot(hidden, w_down, preferred_element_type=jnp.float32), 'he...  12.6 us
    ppermute x5, waiting for transfers between devices, passed_along(): return lax.ppermute(block, axis, route)  5.09 us
    unnamed x48, local copies, waits for them, and re-layouts  4.83 us
  transfers between devices with their start and end apart: 5, of which 1 were waited for; matrix products, arithmetic and copies ran while one was open for 0% of the time, Pallas kernels for 0%

profile of v1, /device:TPU:1, one launch (start us, length us, event | category | flops | bytes accessed | tf_op | source)
XLA Modules:
  0.0 108.6 jit_solution(56641279078006228)
XLA Ops:
  0.7 1.4 %reduce_max.36 = s32[]{:T(128)} reduce(s32[2]{0:T(128)} %param.30, s32[]{:T(128)} %constant.107.clone.1), dimensions={0}, to_apply=%region_0.0 | reduce | flops 1 | bytes 16 | tf_op jit(solution)/shard_map/reduce_max | solution.py:27
  2.7 1.1 %fusion.7 = bf16[2,128]{1,0:T(2,128)(2,1)S(1)} fusion(bf16[2,1024]{1,0:T(2,128)(2,1)} %param.27, bf16[1024,128]{1,0:T(8,128)(2,1)} %param.35), kind=kOutput, calls=%fused_computation.13 | convolution fusion | flops 524800 | bytes 266752 | tf_op jit(solution)/shard_map/dot_general | solution.py:86
  4.0 0.7 copy-done.15
  4.7 0.6 reduce_max.38
  6.3 0.6 broadcast.133.clone
  7.0 0.7 while.52
  7.1 0.6 broadcast_select_fusion.4
  7.9 0.5 copy-done.12
  8.6 0.2 fusion.13
  8.9 0.2 fusion.11
  9.1 0.7 copy-done.5
  10.4 18.8 %psum.21 = f32[2,1024]{1,0:T(2,128)S(1)} all-reduce(f32[2,1024]{1,0:T(2,128)S(1)} %fusion.92), channel_id=1, replica_groups=mesh['req'=64,'head'=8] {'head'}, use_global_device_ids=true, to_apply=%region_8.9 | all-reduce | flops 2048 | bytes 16384 | tf_op jit(solution)/shard_map/psum | solution.py:92
  29.4 0.2 multiply_reduce_fusion.2
  30.2 0.6 broadcast.133
  30.8 0.7 while.53
  30.9 0.6 broadcast_select_fusion.5
  31.5 0.9 fusion.6
  33.1 12.6 %psum.22 = f32[2,1024]{1,0:T(2,128)S(1)} all-reduce(f32[2,1024]{1,0:T(2,128)S(1)} %fusion.94), channel_id=1, replica_groups=mesh['req'=64,'head'=8] {'head'}, use_global_device_ids=true, to_apply=%region_18.19 | all-reduce | flops 2048 | bytes 16384 | tf_op jit(solution)/shard_map/psum | solution.py:98
  45.9 0.2 multiply_reduce_fusion.1
  46.2 0.5 fusion.21
  46.7 12.6 %psum.23 = f32[2,1024]{1,0:T(2,128)S(1)} all-reduce(f32[2,1024]{1,0:T(2,128)S(1)} %fusion.21), channel_id=1, replica_groups=mesh['req'=64,'head'=8] {'head'}, use_global_device_ids=true, to_apply=%region_21.22 | all-reduce | flops 2048 | bytes 16384 | tf_op jit(solution)/shard_map/psum | solution.py:105
  59.5 0.2 multiply_reduce_fusion
  60.5 12.5 %collective-permute-start = (bf16[1,1024]{1,0:T(2,128)(2,1)S(1)}, bf16[1,1024]{1,0:T(2,128)(2,1)S(1)}, u32[]{:S(2)}, u32[]{:S(2)}) collective-permute-start(bf16[1,1024]{1,0:T(2,128)(2,1)S(1)} %constant_dynamic-slice_fusion.4), channel_id=1, source_target_pairs={{256,0},{264,8},{272,16},{280,24},{288,32},{296,40},{304,48},{312,... | collective-permute-start | bytes 6152 | tf_op jit(solution)/shard_map/ppermute | solution.py:12
  73.1 1.9 %collective-permute-start.3 = (bf16[1,512,128]{2,1,0:T(8,128)(2,1)S(1)}, bf16[1,512,128]{2,1,0:T(8,128)(2,1)S(1)}, u32[]{:S(2)}, u32[]{:S(2)}) collective-permute-start(bf16[1,512,128]{2,1,0:T(8,128)(2,1)S(1)} %constant_dynamic-slice_fusion.1), channel_id=1, source_target_pairs={{256,0},{264,8},{272,16},{280,24},{288,32},{296,40},{304,48},{312,... | collective-permute-start | bytes 393224 | tf_op jit(solution)/shard_map/ppermute | solution.py:12
  75.0 12.1 %collective-permute-start.4 = (bf16[1,512,128]{2,1,0:T(8,128)(2,1)S(1)}, bf16[1,512,128]{2,1,0:T(8,128)(2,1)S(1)}, u32[]{:S(2)}, u32[]{:S(2)}) collective-permute-start(bf16[1,512,128]{2,1,0:T(8,128)(2,1)S(1)} %constant_dynamic-slice_fusion), channel_id=1, source_target_pairs={{256,0},{264,8},{272,16},{280,24},{288,32},{296,40},{304,48},{312,... | collective-permute-start | bytes 393224 | tf_op jit(solution)/shard_map/ppermute | solution.py:12
  87.1 1.9 %collective-permute-start.1 = (bf16[1,128]{1,0:T(2,128)(2,1)S(1)}, bf16[1,128]{1,0:T(2,128)(2,1)S(1)}, u32[]{:S(2)}, u32[]{:S(2)}) collective-permute-start(bf16[1,128]{1,0:T(2,128)(2,1)S(1)} %constant_dynamic-slice_fusion.3), channel_id=1, source_target_pairs={{256,0},{264,8},{272,16},{280,24},{288,32},{296,40},{304,48},{312,... | collective-permute-start | bytes 776 | tf_op jit(solution)/shard_map/ppermute | solution.py:12
  89.1 12.1 %collective-permute-start.2 = (bf16[1,128]{1,0:T(2,128)(2,1)S(1)}, bf16[1,128]{1,0:T(2,128)(2,1)S(1)}, u32[]{:S(2)}, u32[]{:S(2)}) collective-permute-start(bf16[1,128]{1,0:T(2,128)(2,1)S(1)} %constant_dynamic-slice_fusion.2), channel_id=1, source_target_pairs={{256,0},{264,8},{272,16},{280,24},{288,32},{296,40},{304,48},{312,... | collective-permute-start | bytes 776 | tf_op jit(solution)/shard_map/ppermute | solution.py:12
  101.2 5.1 %collective-permute-done.1 = bf16[1,128]{1,0:T(2,128)(2,1)S(1)} collective-permute-done((bf16[1,128]{1,0:T(2,128)(2,1)S(1)}, bf16[1,128]{1,0:T(2,128)(2,1)S(1)}, u32[]{:S(2)}, u32[]{:S(2)}) %collective-permute-start.1) | collective-permute-done | bytes 288 | tf_op jit(solution)/shard_map/ppermute | solution.py:12
  106.3 0.5 copy-done.19
  106.8 0.5 copy-done.20
  107.3 0.7 copy.75
  108.0 0.7 copy.76
  (99 shorter events, 4.1 us)
Async XLA Ops:
  0.6 45.6 %copy-start = (bf16[512,1024]{1,0:T(8,128)(2,1)S(1)}, bf16[512,1024]{1,0:T(8,128)(2,1)}, u32[]{:S(2)}) copy-start(bf16[512,1024]{1,0:T(8,128)(2,1)} %param.42) | copy-start | bytes 3145732
  0.6 5.3 %copy-start.2 = (bf16[2,512,128]{2,1,0:T(8,128)(2,1)S(1)}, bf16[2,512,128]{2,1,0:T(8,128)(2,1)}, u32[]{:S(2)}) copy-start(bf16[2,512,128]{2,1,0:T(8,128)(2,1)} %param.28) | copy-start | bytes 786436
  4.0 0.7 copy-start.15
  6.1 1.5 %copy-start.4 = (bf16[1024,128]{1,0:T(8,128)(2,1)S(1)}, bf16[1024,128]{1,0:T(8,128)(2,1)}, u32[]{:S(2)}) copy-start(bf16[1024,128]{1,0:T(8,128)(2,1)} %param.36) | copy-start | bytes 786436
  6.3 1.4 %copy-start.11 = (bf16[2,1024]{1,0:T(2,128)(2,1)S(1)}, bf16[2,1024]{1,0:T(2,128)(2,1)}, u32[]{:S(2)}) copy-start(bf16[2,1024]{1,0:T(2,128)(2,1)} %param.27) | copy-start | bytes 12292
  6.3 0.7 copy-start.14
  7.0 1.8 %copy-start.3 = (bf16[2,512,128]{2,1,0:T(8,128)(2,1)S(1)}, bf16[2,512,128]{2,1,0:T(8,128)(2,1)}, u32[]{:S(2)}) copy-start(bf16[2,512,128]{2,1,0:T(8,128)(2,1)} %param.29) | copy-start | bytes 786436
  7.7 0.7 copy-start.12
  8.9 1.0 copy-start.5
  9.1 1.2 %copy-start.6 = (bf16[128,1024]{1,0:T(8,128)(2,1)S(1)}, bf16[128,1024]{1,0:T(8,128)(2,1)}, u32[]{:S(2)}) copy-start(bf16[128,1024]{1,0:T(8,128)(2,1)} %param.38) | copy-start | bytes 786436
  9.8 19.7 %copy-start.16 = (f32[1024]{0:T(1024)S(1)}, f32[1024]{0:T(1024)}, u32[]{:S(2)}) copy-start(f32[1024]{0:T(1024)} %param.43) | copy-start | bytes 12292
  9.9 19.8 %copy-start.7 = (bf16[1024,128]{1,0:T(8,128)(2,1)S(1)}, bf16[1024,128]{1,0:T(8,128)(2,1)}, u32[]{:S(2)}) copy-start(bf16[1024,128]{1,0:T(8,128)(2,1)} %param.39) | copy-start | bytes 786436
  10.3 19.6 %copy-start.8 = (bf16[2,512,128]{2,1,0:T(8,128)(2,1)S(1)}, bf16[2,512,128]{2,1,0:T(8,128)(2,1)}, u32[]{:S(2)}) copy-start(bf16[2,512,128]{2,1,0:T(8,128)(2,1)} %param.31) | copy-start | bytes 786436
  29.9 2.6 %copy-start.9 = (bf16[2,512,128]{2,1,0:T(8,128)(2,1)S(1)}, bf16[2,512,128]{2,1,0:T(8,128)(2,1)}, u32[]{:S(2)}) copy-start(bf16[2,512,128]{2,1,0:T(8,128)(2,1)} %param.32) | copy-start | bytes 786436
  29.9 3.1 %copy-start.10 = (bf16[128,1024]{1,0:T(8,128)(2,1)S(1)}, bf16[128,1024]{1,0:T(8,128)(2,1)}, u32[]{:S(2)}) copy-start(bf16[128,1024]{1,0:T(8,128)(2,1)} %param.40) | copy-start | bytes 786436
  30.0 16.2 %copy-start.1 = (bf16[1024,512]{1,0:T(8,128)(2,1)S(1)}, bf16[1024,512]{1,0:T(8,128)(2,1)}, u32[]{:S(2)}) copy-start(bf16[1024,512]{1,0:T(8,128)(2,1)} %param.41) | copy-start | bytes 3145732
  33.0 13.2 %copy-start.17 = (f32[1024]{0:T(1024)S(1)}, f32[1024]{0:T(1024)}, u32[]{:S(2)}) copy-start(f32[1024]{0:T(1024)} %param.44) | copy-start | bytes 12292
  59.7 0.7 copy-start.18
  60.5 46.3 %collective-permute-start = (bf16[1,1024]{1,0:T(2,128)(2,1)S(1)}, bf16[1,1024]{1,0:T(2,128)(2,1)S(1)}, u32[]{:S(2)}, u32[]{:S(2)}) collective-permute-start(bf16[1,1024]{1,0:T(2,128)(2,1)S(1)} %constant_dynamic-slice_fusion.4), channel_id=1, source_target_pairs={{256,0},{264,8},{272,16},{280,24},{288,32},{296,40},{304,48},{312,... | collective-permute-start | bytes 6152 | tf_op jit(solution)/shard_map/ppermute | solution.py:12
  73.1 34.2 %collective-permute-start.3 = (bf16[1,512,128]{2,1,0:T(8,128)(2,1)S(1)}, bf16[1,512,128]{2,1,0:T(8,128)(2,1)S(1)}, u32[]{:S(2)}, u32[]{:S(2)}) collective-permute-start(bf16[1,512,128]{2,1,0:T(8,128)(2,1)S(1)} %constant_dynamic-slice_fusion.1), channel_id=1, source_target_pairs={{256,0},{264,8},{272,16},{280,24},{288,32},{296,40},{304,48},{312,... | collective-permute-start | bytes 393224 | tf_op jit(solution)/shard_map/ppermute | solution.py:12
  75.0 32.3 %collective-permute-start.4 = (bf16[1,512,128]{2,1,0:T(8,128)(2,1)S(1)}, bf16[1,512,128]{2,1,0:T(8,128)(2,1)S(1)}, u32[]{:S(2)}, u32[]{:S(2)}) collective-permute-start(bf16[1,512,128]{2,1,0:T(8,128)(2,1)S(1)} %constant_dynamic-slice_fusion), channel_id=1, source_target_pairs={{256,0},{264,8},{272,16},{280,24},{288,32},{296,40},{304,48},{312,... | collective-permute-start | bytes 393224 | tf_op jit(solution)/shard_map/ppermute | solution.py:12
  87.1 19.1 %collective-permute-start.1 = (bf16[1,128]{1,0:T(2,128)(2,1)S(1)}, bf16[1,128]{1,0:T(2,128)(2,1)S(1)}, u32[]{:S(2)}, u32[]{:S(2)}) collective-permute-start(bf16[1,128]{1,0:T(2,128)(2,1)S(1)} %constant_dynamic-slice_fusion.3), channel_id=1, source_target_pairs={{256,0},{264,8},{272,16},{280,24},{288,32},{296,40},{304,48},{312,... | collective-permute-start | bytes 776 | tf_op jit(solution)/shard_map/ppermute | solution.py:12
  89.1 17.2 %collective-permute-start.2 = (bf16[1,128]{1,0:T(2,128)(2,1)S(1)}, bf16[1,128]{1,0:T(2,128)(2,1)S(1)}, u32[]{:S(2)}, u32[]{:S(2)}) collective-permute-start(bf16[1,128]{1,0:T(2,128)(2,1)S(1)} %constant_dynamic-slice_fusion.2), channel_id=1, source_target_pairs={{256,0},{264,8},{272,16},{280,24},{288,32},{296,40},{304,48},{312,... | collective-permute-start | bytes 776 | tf_op jit(solution)/shard_map/ppermute | solution.py:12
  106.3 0.5 copy-start.19
  106.8 0.5 copy-start.20
  107.3 0.7 copy-start.13

commit v2 on v1

--- a/solution.py
+++ b/solution.py
@@ -10,6 +10,18 @@
     devices = range(lax.axis_size(axis))
     route = [((i - distance) % len(devices), i) for i in devices]
     return lax.ppermute(block, axis, route)
+
+
+def head_sum(value):
+    count = lax.axis_size("head")
+    if count & (count - 1):
+        return lax.psum(value, "head")
+    stride = 1
+    while stride < count:
+        route = [(i, i ^ stride) for i in range(count)]
+        value = value + lax.ppermute(value, "head", route)
+        stride *= 2
+    return value
 
 
 def layer_norm(value, gain):
@@ -89,20 +101,20 @@
     fresh_keys = jnp.dot(tokens, w_key, preferred_element_type=jnp.float32).astype(jnp.bfloat16)
     fresh_values = jnp.dot(tokens, w_value, preferred_element_type=jnp.float32).astype(jnp.bfloat16)
     self_mixed = attend(query, self_keys, self_values, self_len, fresh_keys, fresh_values)
-    self_total = lax.psum(jnp.dot(self_mixed, w_out, preferred_element_type=jnp.float32), "head")
+    self_total = head_sum(jnp.dot(self_mixed, w_out, preferred_element_type=jnp.float32))
     first = layer_norm(tokens.astype(jnp.float32) + self_total, gain_self).astype(jnp.bfloat16)
     cross_query = (
         jnp.dot(first, w_cross_query, preferred_element_type=jnp.float32) * scale
     ).astype(jnp.bfloat16)
     cross_mixed = attend(cross_query, cross_keys, cross_values, cross_len, None, None)
-    cross_total = lax.psum(
-        jnp.dot(cross_mixed, w_cross_out, preferred_element_type=jnp.float32), "head"
+    cross_total = head_sum(
+        jnp.dot(cross_mixed, w_cross_out, preferred_element_type=jnp.float32)
     )
     second = layer_norm(first.astype(jnp.float32) + cross_total, gain_cross).astype(jnp.bfloat16)
     hidden = jax.nn.gelu(
         jnp.dot(second, w_up, preferred_element_type=jnp.float32), approximate=False
     ).astype(jnp.bfloat16)
-    ffn_total = lax.psum(jnp.dot(hidden, w_down, preferred_element_type=jnp.float32), "head")
+    ffn_total = head_sum(jnp.dot(hidden, w_down, preferred_element_type=jnp.float32))
     layer_out = layer_norm(second.astype(jnp.float32) + ffn_total, gain_final).astype(jnp.bfloat16)
     return (layer_out, fresh_keys, fresh_values)
 
@@ -151,24 +163,26 @@
     )
     chosen = give_slot[0]
     half_axis = lax.axis_size("req") // 2
-    moved_keys, moved_values = passed_along(
-        (take_slot(self_keys, chosen), take_slot(self_values, chosen)), "req", half_axis
-    )
+    caches = jnp.concatenate((take_slot(self_keys, chosen), take_slot(self_values, chosen)), axis=0)
+    moved = passed_along(caches, "req", half_axis)
+    moved_keys, moved_values = moved[:1], moved[1:]
     layer_out, fresh_keys, fresh_values = decode_layer(
         tokens, self_keys, self_values, self_len, cross_keys, cross_values, cross_len, params
     )
-    arrived = passed_along(
+    width = layer_out.shape[1]
+    part = fresh_keys.shape[1]
+    rows = jnp.concatenate(
         (
             take_slot(layer_out, chosen),
             take_slot(fresh_keys, chosen),
             take_slot(fresh_values, chosen),
         ),
-        "req",
-        half_axis,
-    )
-    decoded = put_slot(layer_out, arrived[0], chosen)
-    new_keys = put_slot(fresh_keys, arrived[1], chosen)
-    new_values = put_slot(fresh_values, arrived[2], chosen)
+        axis=1,
+    )
+    arrived = passed_along(rows, "req", half_axis)
+    decoded = put_slot(layer_out, arrived[:, :width], chosen)
+    new_keys = put_slot(fresh_keys, arrived[:, width : width + part], chosen)
+    new_values = put_slot(fresh_values, arrived[:, width + part :], chosen)
     return (decoded, new_keys, new_values, moved_keys, moved_values)
 
 

time: 109 us -> 99.6 us (0.914)
  the two profiles are of different devices: /device:TPU:1 before, /device:TPU:6 now
where the time goes in v2:
time: 99.6 us; the launch traced here: 98.9 us
  starting transfers between devices  47.9 us (48%)
  waiting for transfers between devices  31 us (31%)
  local copies, waits for them, and re-layouts  6.86 us (7%)
  other arithmetic  6.19 us (6%)
  matrix products  4.02 us (4%)
  between operations  3.01 us (3%)
    ppermute x9, starting transfers between devices, head_sum(): value = value + lax.ppermute(value, 'head', route)  29.7 us
    ppermute x2, waiting for transfers between devices, passed_along(): return lax.ppermute(block, axis, route)  19 us
    ppermute x2, starting transfers between devices, passed_along(): return lax.ppermute(block, axis, route)  18.2 us
    ppermute x9, waiting for transfers between devices, head_sum(): value = value + lax.ppermute(value, 'head', route)  12 us
    unnamed x44, local copies, waits for them, and re-layouts  4.13 us
    reduce_max x2, other arithmetic, attend(): steps = (jnp.max(lengths) + block - 1) // block  2.03 us
  transfers between devices with their start and end apart: 11, of which 8 were waited for; matrix products, arithmetic and copies ran while one was open for 2% of the time, Pallas kernels for 0%

profile of v2, /device:TPU:6, one launch (start us, length us, event | category | flops | bytes accessed | tf_op | source)
XLA Modules:
  0.0 98.9 jit_solution(7885738447161976229)
XLA Ops:
  0.7 1.4 %reduce_max.36 = s32[]{:T(128)} reduce(s32[2]{0:T(128)} %param.30, s32[]{:T(128)} %constant.107.clone.1), dimensions={0}, to_apply=%region_0.0 | reduce | flops 1 | bytes 16 | tf_op jit(solution)/shard_map/reduce_max | solution.py:39
  2.7 1.1 %fusion.7 = bf16[2,128]{1,0:T(2,128)(2,1)S(1)} fusion(bf16[2,1024]{1,0:T(2,128)(2,1)} %param.27, bf16[1024,128]{1,0:T(8,128)(2,1)} %param.35), kind=kOutput, calls=%fused_computation.13 | convolution fusion | flops 524800 | bytes 266752 | tf_op jit(solution)/shard_map/dot_general | solution.py:98
  5.0 0.7 while.52
  5.1 0.6 broadcast_select_fusion.4
  7.1 0.7 copy-done.5
  8.4 1.9 %collective-permute-start = (f32[2,1024]{1,0:T(2,128)S(1)}, f32[2,1024]{1,0:T(2,128)S(1)}, u32[]{:S(2)}, u32[]{:S(2)}) collective-permute-start(f32[2,1024]{1,0:T(2,128)S(1)} %fusion.93), channel_id=1, source_target_pairs={{0,1},{1,0},{2,3},{3,2},{4,5},{5,4},{6,7},{7,6},{8,9},{9,8},{10,11... | collective-permute-start | bytes 24584 | tf_op jit(solution)/shard_map/ppermute | solution.py:22
  10.4 1.1 %collective-permute-done = f32[2,1024]{1,0:T(2,128)S(1)} collective-permute-done((f32[2,1024]{1,0:T(2,128)S(1)}, f32[2,1024]{1,0:T(2,128)S(1)}, u32[]{:S(2)}, u32[]{:S(2)}) %collective-permute-start) | collective-permute-done | bytes 8224 | tf_op jit(solution)/shard_map/ppermute | solution.py:22
  11.5 3.5 %collective-permute-start.1 = (f32[2,1024]{1,0:T(2,128)S(1)}, f32[2,1024]{1,0:T(2,128)S(1)}, u32[]{:S(2)}, u32[]{:S(2)}) collective-permute-start(f32[2,1024]{1,0:T(2,128)S(1)} %add.146), channel_id=1, source_target_pairs={{0,2},{1,3},{2,0},{3,1},{4,6},{5,7},{6,4},{7,5},{8,10},{9,11},{10,... | collective-permute-start | bytes 24584 | tf_op jit(solution)/shard_map/ppermute | solution.py:22
  15.0 2.1 %collective-permute-done.1 = f32[2,1024]{1,0:T(2,128)S(1)} collective-permute-done((f32[2,1024]{1,0:T(2,128)S(1)}, f32[2,1024]{1,0:T(2,128)S(1)}, u32[]{:S(2)}, u32[]{:S(2)}) %collective-permute-start.1) | collective-permute-done | bytes 8224 | tf_op jit(solution)/shard_map/ppermute | solution.py:22
  17.1 5.1 %collective-permute-start.2 = (f32[2,1024]{1,0:T(2,128)S(1)}, f32[2,1024]{1,0:T(2,128)S(1)}, u32[]{:S(2)}, u32[]{:S(2)}) collective-permute-start(f32[2,1024]{1,0:T(2,128)S(1)} %add.147), channel_id=1, source_target_pairs={{0,4},{1,5},{2,6},{3,7},{4,0},{5,1},{6,2},{7,3},{8,12},{9,13},{10,... | collective-permute-start | bytes 24584 | tf_op jit(solution)/shard_map/ppermute | solution.py:22
  22.2 0.6 reduce_max.38
  23.7 0.8 copy-done.8
  24.9 1.2 %fusion.8 = bf16[2,128]{1,0:T(2,128)(2,1)S(1)} fusion(bf16[1024,128]{1,0:T(8,128)(2,1)} %param.39, f32[2,1024]{1,0:T(2,128)S(1)} %get-tuple-element.358, f32[2]{0:T(128)S(1)} %add_rsqrt_fusion.2, f32[2]{0:T(128)S(1)} %broadcast_multiply_fusion.2, f32[1024]{0:T(1024)S(1)} %copy-done.18), kind=kOutput, calls=%fused_computation.14 | convolution fusion | flops 532992 | bytes 274960 | tf_op jit(solution)/shard_map/dot_general | solution.py:107
  26.3 0.6 broadcast.133
  27.0 0.7 while.53
  27.0 0.6 broadcast_select_fusion.5
  27.6 0.9 fusion.6
  29.1 1.9 %collective-permute-start.3 = (f32[2,1024]{1,0:T(2,128)S(1)}, f32[2,1024]{1,0:T(2,128)S(1)}, u32[]{:S(2)}, u32[]{:S(2)}) collective-permute-start(f32[2,1024]{1,0:T(2,128)S(1)} %fusion.95), channel_id=1, source_target_pairs={{0,1},{1,0},{2,3},{3,2},{4,5},{5,4},{6,7},{7,6},{8,9},{9,8},{10,11... | collective-permute-start | bytes 24584 | tf_op jit(solution)/shard_map/ppermute | solution.py:22
  31.0 1.1 %collective-permute-done.3 = f32[2,1024]{1,0:T(2,128)S(1)} collective-permute-done((f32[2,1024]{1,0:T(2,128)S(1)}, f32[2,1024]{1,0:T(2,128)S(1)}, u32[]{:S(2)}, u32[]{:S(2)}) %collective-permute-start.3) | collective-permute-done | bytes 8224 | tf_op jit(solution)/shard_map/ppermute | solution.py:22
  32.2 3.0 %collective-permute-start.4 = (f32[2,1024]{1,0:T(2,128)S(1)}, f32[2,1024]{1,0:T(2,128)S(1)}, u32[]{:S(2)}, u32[]{:S(2)}) collective-permute-start(f32[2,1024]{1,0:T(2,128)S(1)} %add.151), channel_id=1, source_target_pairs={{0,2},{1,3},{2,0},{3,1},{4,6},{5,7},{6,4},{7,5},{8,10},{9,11},{10,... | collective-permute-start | bytes 24584 | tf_op jit(solution)/shard_map/ppermute | solution.py:22
  35.2 2.6 %collective-permute-done.4 = f32[2,1024]{1,0:T(2,128)S(1)} collective-permute-done((f32[2,1024]{1,0:T(2,128)S(1)}, f32[2,1024]{1,0:T(2,128)S(1)}, u32[]{:S(2)}, u32[]{:S(2)}) %collective-permute-start.4) | collective-permute-done | bytes 8224 | tf_op jit(solution)/shard_map/ppermute | solution.py:22
  37.7 4.6 %collective-permute-start.5 = (f32[2,1024]{1,0:T(2,128)S(1)}, f32[2,1024]{1,0:T(2,128)S(1)}, u32[]{:S(2)}, u32[]{:S(2)}) collective-permute-start(f32[2,1024]{1,0:T(2,128)S(1)} %add.152), channel_id=1, source_target_pairs={{0,4},{1,5},{2,6},{3,7},{4,0},{5,1},{6,2},{7,3},{8,12},{9,13},{10,... | collective-permute-start | bytes 24584 | tf_op jit(solution)/shard_map/ppermute | solution.py:22
  43.0 1.8 %collective-permute-done.5 = f32[2,1024]{1,0:T(2,128)S(1)} collective-permute-done((f32[2,1024]{1,0:T(2,128)S(1)}, f32[2,1024]{1,0:T(2,128)S(1)}, u32[]{:S(2)}, u32[]{:S(2)}) %collective-permute-start.5) | collective-permute-done | bytes 8224 | tf_op jit(solution)/shard_map/ppermute | solution.py:22
  46.2 1.9 %collective-permute-start.6 = (f32[2,1024]{1,0:T(2,128)S(1)}, f32[2,1024]{1,0:T(2,128)S(1)}, u32[]{:S(2)}, u32[]{:S(2)}) collective-permute-start(f32[2,1024]{1,0:T(2,128)S(1)} %fusion.21), channel_id=1, source_target_pairs={{0,1},{1,0},{2,3},{3,2},{4,5},{5,4},{6,7},{7,6},{8,9},{9,8},{10,11... | collective-permute-start | bytes 24584 | tf_op jit(solution)/shard_map/ppermute | solution.py:22
  48.1 1.1 %collective-permute-done.6 = f32[2,1024]{1,0:T(2,128)S(1)} collective-permute-done((f32[2,1024]{1,0:T(2,128)S(1)}, f32[2,1024]{1,0:T(2,128)S(1)}, u32[]{:S(2)}, u32[]{:S(2)}) %collective-permute-start.6) | collective-permute-done | bytes 8224 | tf_op jit(solution)/shard_map/ppermute | solution.py:22
  49.3 3.0 %collective-permute-start.7 = (f32[2,1024]{1,0:T(2,128)S(1)}, f32[2,1024]{1,0:T(2,128)S(1)}, u32[]{:S(2)}, u32[]{:S(2)}) collective-permute-start(f32[2,1024]{1,0:T(2,128)S(1)} %add.156), channel_id=1, source_target_pairs={{0,2},{1,3},{2,0},{3,1},{4,6},{5,7},{6,4},{7,5},{8,10},{9,11},{10,... | collective-permute-start | bytes 24584 | tf_op jit(solution)/shard_map/ppermute | solution.py:22
  52.3 15.7 %collective-permute-start.10 = (bf16[2,512,128]{2,1,0:T(8,128)(2,1)S(1)}, bf16[2,512,128]{2,1,0:T(8,128)(2,1)S(1)}, u32[]{:S(2)}, u32[]{:S(2)}) collective-permute-start(bf16[2,512,128]{2,1,0:T(8,128)(2,1)S(1)} %pad_maximum_fusion), channel_id=1, source_target_pairs={{256,0},{264,8},{272,16},{280,24},{288,32},{296,40},{304,48},{312,... | collective-permute-start | bytes 786440 | tf_op jit(solution)/shard_map/ppermute | solution.py:12
  68.0 4.8 %collective-permute-start.8 = (f32[2,1024]{1,0:T(2,128)S(1)}, f32[2,1024]{1,0:T(2,128)S(1)}, u32[]{:S(2)}, u32[]{:S(2)}) collective-permute-start(f32[2,1024]{1,0:T(2,128)S(1)} %add.157), channel_id=1, source_target_pairs={{0,4},{1,5},{2,6},{3,7},{4,0},{5,1},{6,2},{7,3},{8,12},{9,13},{10,... | collective-permute-start | bytes 24584 | tf_op jit(solution)/shard_map/ppermute | solution.py:22
  72.9 2.2 %collective-permute-done.8 = f32[2,1024]{1,0:T(2,128)S(1)} collective-permute-done((f32[2,1024]{1,0:T(2,128)S(1)}, f32[2,1024]{1,0:T(2,128)S(1)}, u32[]{:S(2)}, u32[]{:S(2)}) %collective-permute-start.8) | collective-permute-done | bytes 8224 | tf_op jit(solution)/shard_map/ppermute | solution.py:22
  76.1 2.5 %collective-permute-start.9 = (bf16[1,1280]{1,0:T(2,128)(2,1)S(1)}, bf16[1,1280]{1,0:T(2,128)(2,1)S(1)}, u32[]{:S(2)}, u32[]{:S(2)}) collective-permute-start(bf16[1,1280]{1,0:T(2,128)(2,1)S(1)} %pad_maximum_fusion.1), channel_id=1, source_target_pairs={{256,0},{264,8},{272,16},{280,24},{288,32},{296,40},{304,48},{312,... | collective-permute-start | bytes 7688 | tf_op jit(solution)/shard_map/ppermute | solution.py:12
  78.6 19.0 %collective-permute-done.9 = bf16[1,1280]{1,0:T(2,128)(2,1)S(1)} collective-permute-done((bf16[1,1280]{1,0:T(2,128)(2,1)S(1)}, bf16[1,1280]{1,0:T(2,128)(2,1)S(1)}, u32[]{:S(2)}, u32[]{:S(2)}) %collective-permute-start.9) | collective-permute-done | bytes 2592 | tf_op jit(solution)/shard_map/ppermute | solution.py:12
  98.2 0.7 fusion.89
  (111 shorter events, 7.9 us)
Async XLA Ops:
  0.6 44.5 %copy-start = (bf16[512,1024]{1,0:T(8,128)(2,1)S(1)}, bf16[512,1024]{1,0:T(8,128)(2,1)}, u32[]{:S(2)}) copy-start(bf16[512,1024]{1,0:T(8,128)(2,1)} %param.42) | copy-start | bytes 3145732
  0.6 3.4 %copy-start.3 = (bf16[2,512,128]{2,1,0:T(8,128)(2,1)S(1)}, bf16[2,512,128]{2,1,0:T(8,128)(2,1)}, u32[]{:S(2)}) copy-start(bf16[2,512,128]{2,1,0:T(8,128)(2,1)} %param.28) | copy-start | bytes 786436
  4.2 1.5 %copy-start.4 = (bf16[1024,128]{1,0:T(8,128)(2,1)S(1)}, bf16[1024,128]{1,0:T(8,128)(2,1)}, u32[]{:S(2)}) copy-start(bf16[1024,128]{1,0:T(8,128)(2,1)} %param.36) | copy-start | bytes 786436
  4.3 1.4 %copy-start.11 = (bf16[2,1024]{1,0:T(2,128)(2,1)S(1)}, bf16[2,1024]{1,0:T(2,128)(2,1)}, u32[]{:S(2)}) copy-start(bf16[2,1024]{1,0:T(2,128)(2,1)} %param.27) | copy-start | bytes 12292
  4.3 0.7 copy-start.14
  5.0 1.8 %copy-start.2 = (bf16[2,512,128]{2,1,0:T(8,128)(2,1)S(1)}, bf16[2,512,128]{2,1,0:T(8,128)(2,1)}, u32[]{:S(2)}) copy-start(bf16[2,512,128]{2,1,0:T(8,128)(2,1)} %param.29) | copy-start | bytes 786436
  5.7 0.7 copy-start.10
  6.9 1.0 copy-start.5
  7.1 1.2 %copy-start.6 = (bf16[128,1024]{1,0:T(8,128)(2,1)S(1)}, bf16[128,1024]{1,0:T(8,128)(2,1)}, u32[]{:S(2)}) copy-start(bf16[128,1024]{1,0:T(8,128)(2,1)} %param.38) | copy-start | bytes 786436
  7.9 15.6 %copy-start.7 = (bf16[2,512,128]{2,1,0:T(8,128)(2,1)S(1)}, bf16[2,512,128]{2,1,0:T(8,128)(2,1)}, u32[]{:S(2)}) copy-start(bf16[2,512,128]{2,1,0:T(8,128)(2,1)} %param.31) | copy-start | bytes 786436
  8.4 3.1 %collective-permute-start = (f32[2,1024]{1,0:T(2,128)S(1)}, f32[2,1024]{1,0:T(2,128)S(1)}, u32[]{:S(2)}, u32[]{:S(2)}) collective-permute-start(f32[2,1024]{1,0:T(2,128)S(1)} %fusion.93), channel_id=1, source_target_pairs={{0,1},{1,0},{2,3},{3,2},{4,5},{5,4},{6,7},{7,6},{8,9},{9,8},{10,11... | collective-permute-start | bytes 24584 | tf_op jit(solution)/shard_map/ppermute | solution.py:22
  11.5 10.7 %copy-start.15 = (s32[2]{0:T(128)S(1)}, s32[2]{0:T(128)}, u32[]{:S(2)}) copy-start(s32[2]{0:T(128)} %param.33) | copy-start | bytes 28
  11.5 5.5 %collective-permute-start.1 = (f32[2,1024]{1,0:T(2,128)S(1)}, f32[2,1024]{1,0:T(2,128)S(1)}, u32[]{:S(2)}, u32[]{:S(2)}) collective-permute-start(f32[2,1024]{1,0:T(2,128)S(1)} %add.146), channel_id=1, source_target_pairs={{0,2},{1,3},{2,0},{3,1},{4,6},{5,7},{6,4},{7,5},{8,10},{9,11},{10,... | collective-permute-start | bytes 24584 | tf_op jit(solution)/shard_map/ppermute | solution.py:22
  17.1 7.5 %collective-permute-start.2 = (f32[2,1024]{1,0:T(2,128)S(1)}, f32[2,1024]{1,0:T(2,128)S(1)}, u32[]{:S(2)}, u32[]{:S(2)}) collective-permute-start(f32[2,1024]{1,0:T(2,128)S(1)} %add.147), channel_id=1, source_target_pairs={{0,4},{1,5},{2,6},{3,7},{4,0},{5,1},{6,2},{7,3},{8,12},{9,13},{10,... | collective-permute-start | bytes 24584 | tf_op jit(solution)/shard_map/ppermute | solution.py:22
  23.5 1.0 copy-start.8
  23.5 1.4 %copy-start.18 = (f32[1024]{0:T(1024)S(1)}, f32[1024]{0:T(1024)}, u32[]{:S(2)}) copy-start(f32[1024]{0:T(1024)} %param.43) | copy-start | bytes 12292
  24.4 20.8 %copy-start.1 = (bf16[1024,512]{1,0:T(8,128)(2,1)S(1)}, bf16[1024,512]{1,0:T(8,128)(2,1)}, u32[]{:S(2)}) copy-start(bf16[1024,512]{1,0:T(8,128)(2,1)} %param.41) | copy-start | bytes 3145732
  27.6 1.3 %copy-start.9 = (bf16[128,1024]{1,0:T(8,128)(2,1)S(1)}, bf16[128,1024]{1,0:T(8,128)(2,1)}, u32[]{:S(2)}) copy-start(bf16[128,1024]{1,0:T(8,128)(2,1)} %param.40) | copy-start | bytes 786436
  29.1 3.1 %collective-permute-start.3 = (f32[2,1024]{1,0:T(2,128)S(1)}, f32[2,1024]{1,0:T(2,128)S(1)}, u32[]{:S(2)}, u32[]{:S(2)}) collective-permute-start(f32[2,1024]{1,0:T(2,128)S(1)} %fusion.95), channel_id=1, source_target_pairs={{0,1},{1,0},{2,3},{3,2},{4,5},{5,4},{6,7},{7,6},{8,9},{9,8},{10,11... | collective-permute-start | bytes 24584 | tf_op jit(solution)/shard_map/ppermute | solution.py:22
  32.2 5.5 %collective-permute-start.4 = (f32[2,1024]{1,0:T(2,128)S(1)}, f32[2,1024]{1,0:T(2,128)S(1)}, u32[]{:S(2)}, u32[]{:S(2)}) collective-permute-start(f32[2,1024]{1,0:T(2,128)S(1)} %add.151), channel_id=1, source_target_pairs={{0,2},{1,3},{2,0},{3,1},{4,6},{5,7},{6,4},{7,5},{8,10},{9,11},{10,... | collective-permute-start | bytes 24584 | tf_op jit(solution)/shard_map/ppermute | solution.py:22
  37.7 7.0 %collective-permute-start.5 = (f32[2,1024]{1,0:T(2,128)S(1)}, f32[2,1024]{1,0:T(2,128)S(1)}, u32[]{:S(2)}, u32[]{:S(2)}) collective-permute-start(f32[2,1024]{1,0:T(2,128)S(1)} %add.152), channel_id=1, source_target_pairs={{0,4},{1,5},{2,6},{3,7},{4,0},{5,1},{6,2},{7,3},{8,12},{9,13},{10,... | collective-permute-start | bytes 24584 | tf_op jit(solution)/shard_map/ppermute | solution.py:22
  45.0 0.7 copy-start.12
  46.2 3.1 %collective-permute-start.6 = (f32[2,1024]{1,0:T(2,128)S(1)}, f32[2,1024]{1,0:T(2,128)S(1)}, u32[]{:S(2)}, u32[]{:S(2)}) collective-permute-start(f32[2,1024]{1,0:T(2,128)S(1)} %fusion.21), channel_id=1, source_target_pairs={{0,1},{1,0},{2,3},{3,2},{4,5},{5,4},{6,7},{7,6},{8,9},{9,8},{10,11... | collective-permute-start | bytes 24584 | tf_op jit(solution)/shard_map/ppermute | solution.py:22
  49.3 18.7 %collective-permute-start.7 = (f32[2,1024]{1,0:T(2,128)S(1)}, f32[2,1024]{1,0:T(2,128)S(1)}, u32[]{:S(2)}, u32[]{:S(2)}) collective-permute-start(f32[2,1024]{1,0:T(2,128)S(1)} %add.156), channel_id=1, source_target_pairs={{0,2},{1,3},{2,0},{3,1},{4,6},{5,7},{6,4},{7,5},{8,10},{9,11},{10,... | collective-permute-start | bytes 24584 | tf_op jit(solution)/shard_map/ppermute | solution.py:22
  52.3 45.9 %collective-permute-start.10 = (bf16[2,512,128]{2,1,0:T(8,128)(2,1)S(1)}, bf16[2,512,128]{2,1,0:T(8,128)(2,1)S(1)}, u32[]{:S(2)}, u32[]{:S(2)}) collective-permute-start(bf16[2,512,128]{2,1,0:T(8,128)(2,1)S(1)} %pad_maximum_fusion), channel_id=1, source_target_pairs={{256,0},{264,8},{272,16},{280,24},{288,32},{296,40},{304,48},{312,... | collective-permute-start | bytes 786440 | tf_op jit(solution)/shard_map/ppermute | solution.py:12
  68.0 7.0 %collective-permute-start.8 = (f32[2,1024]{1,0:T(2,128)S(1)}, f32[2,1024]{1,0:T(2,128)S(1)}, u32[]{:S(2)}, u32[]{:S(2)}) collective-permute-start(f32[2,1024]{1,0:T(2,128)S(1)} %add.157), channel_id=1, source_target_pairs={{0,4},{1,5},{2,6},{3,7},{4,0},{5,1},{6,2},{7,3},{8,12},{9,13},{10,... | collective-permute-start | bytes 24584 | tf_op jit(solution)/shard_map/ppermute | solution.py:22
  75.3 0.7 copy-start.19
  76.1 21.4 %collective-permute-start.9 = (bf16[1,1280]{1,0:T(2,128)(2,1)S(1)}, bf16[1,1280]{1,0:T(2,128)(2,1)S(1)}, u32[]{:S(2)}, u32[]{:S(2)}) collective-permute-start(bf16[1,1280]{1,0:T(2,128)(2,1)S(1)} %pad_maximum_fusion.1), channel_id=1, source_target_pairs={{256,0},{264,8},{272,16},{280,24},{288,32},{296,40},{304,48},{312,... | collective-permute-start | bytes 7688 | tf_op jit(solution)/shard_map/ppermute | solution.py:12
  97.6 0.6 copy-start.13
  97.6 0.5 copy-start.16
  98.2 0.7 copy-start.17

commit v3 on v2

--- a/solution.py
+++ b/solution.py
@@ -14,14 +14,9 @@
 
 def head_sum(value):
     count = lax.axis_size("head")
-    if count & (count - 1):
-        return lax.psum(value, "head")
-    stride = 1
-    while stride < count:
-        route = [(i, i ^ stride) for i in range(count)]
-        value = value + lax.ppermute(value, "head", route)
-        stride *= 2
-    return value
+    spread = jnp.broadcast_to(value[None], (count,) + value.shape)
+    gathered = lax.all_to_all(spread, "head", 0, 0)
+    return jnp.sum(gathered, axis=0)
 
 
 def layer_norm(value, gain):

time: 99.6 us -> 75.2 us (0.76)
  the two profiles are of different devices: /device:TPU:6 before, /device:TPU:8 now
where the time goes in v3:
time: 75.2 us; the launch traced here: 74.5 us
  starting transfers between devices  34.2 us (45%)
  waiting for transfers between devices  18.7 us (25%)
  local copies, waits for them, and re-layouts  9.44 us (13%)
  other arithmetic  6.26 us (8%)
  matrix products  2.98 us (4%)
  between operations  2.92 us (4%)
    all_to_all x3, starting transfers between devices, head_sum(): gathered = lax.all_to_all(spread, 'head', 0, 0)  18.6 us
    ppermute x2, starting transfers between devices, passed_along(): return lax.ppermute(block, axis, route)  15.6 us
    ppermute x2, waiting for transfers between devices, passed_along(): return lax.ppermute(block, axis, route)  14 us
    unnamed x46, local copies, waits for them, and re-layouts  4.75 us
    all_to_all x3, waiting for transfers between devices, head_sum(): gathered = lax.all_to_all(spread, 'head', 0, 0)  4.62 us
    reduce_max x2, other arithmetic, attend(): steps = (jnp.max(lengths) + block - 1) // block  2.03 us
    broadcast_in_dim x3, local copies, waits for them, and re-layouts, head_sum(): spread = jnp.broadcast_to(value[None], (count,) + value.shape)  1.97 us
  transfers between devices with their start and end apart: 5, of which 3 were waited for; matrix products, arithmetic and copies ran while one was open for 4% of the time, Pallas kernels for 0%

profile of v3, /device:TPU:8, one launch (start us, length us, event | category | flops | bytes accessed | tf_op | source)
XLA Modules:
  0.0 74.5 jit_solution(7975579399525508833)
XLA Ops:
  0.7 1.4 %reduce_max.36 = s32[]{:T(128)} reduce(s32[2]{0:T(128)} %param.30, s32[]{:T(128)} %constant.107.clone.1), dimensions={0}, to_apply=%region_0.0 | reduce | flops 1 | bytes 16 | tf_op jit(solution)/shard_map/reduce_max | solution.py:34
  2.7 1.1 %fusion.7 = bf16[2,128]{1,0:T(2,128)(2,1)S(1)} fusion(bf16[2,1024]{1,0:T(2,128)(2,1)} %param.27, bf16[1024,128]{1,0:T(8,128)(2,1)} %param.35), kind=kOutput, calls=%fused_computation.13 | convolution fusion | flops 524800 | bytes 266752 | tf_op jit(solution)/shard_map/dot_general | solution.py:93
  4.4 0.6 broadcast.136.clone
  5.0 0.7 while.52
  5.1 0.6 broadcast_select_fusion.4
  5.9 0.5 copy-done.12
  7.1 0.7 copy-done.5
  8.4 0.7 broadcast_in_dim.40
  9.1 9.1 %all-to-all-start = ((f32[8,2,1024]{2,1,0:T(2,128)}), f32[8,2,1024]{2,1,0:T(2,128)S(1)}, u32[]{:S(2)}, u32[]{:S(2)}) async-start(f32[8,2,1024]{2,1,0:T(2,128)} %broadcast_in_dim.40), calls=%async_computation | async-start | bytes 131072 | tf_op jit(solution)/shard_map/all_to_all | solution.py:18
  18.9 0.6 copy-done.15
  19.5 0.6 reduce_max.38
  20.9 0.8 %copy-done.8 = bf16[2,512,128]{2,1,0:T(8,128)(2,1)S(1)} copy-done((bf16[2,512,128]{2,1,0:T(8,128)(2,1)S(1)}, bf16[2,512,128]{2,1,0:T(8,128)(2,1)}, u32[]{:S(2)}) %copy-start.8) | copy-done | bytes 262168
  21.9 0.5 all-to-all-done
  22.5 0.2 multiply_reduce_fusion.2
  22.7 0.3 copy-done.18
  23.5 0.6 broadcast.136
  24.1 0.7 while.53
  24.2 0.6 broadcast_select_fusion.5
  24.8 0.9 %fusion.6 = f32[2,2,512]{2,1,0:T(2,128)S(1)} fusion(f32[2,2,512]{2,1,0:T(2,128)} %get-tuple-element.291), kind=kOutput, calls=%fused_computation.10 | output fusion | flops 2563 | bytes 16384 | tf_op jit(solution)/shard_map/sub | solution.py:56
  26.3 0.7 broadcast_in_dim.41
  26.9 4.7 %all-to-all-start.1 = ((f32[8,2,1024]{2,1,0:T(2,128)}), f32[8,2,1024]{2,1,0:T(2,128)S(1)}, u32[]{:S(2)}, u32[]{:S(2)}) async-start(f32[8,2,1024]{2,1,0:T(2,128)} %broadcast_in_dim.41), calls=%async_computation.1 | async-start | bytes 131072 | tf_op jit(solution)/shard_map/all_to_all | solution.py:18
  31.7 11.6 %collective-permute-start.1 = (bf16[2,512,128]{2,1,0:T(8,128)(2,1)S(1)}, bf16[2,512,128]{2,1,0:T(8,128)(2,1)S(1)}, u32[]{:S(2)}, u32[]{:S(2)}) collective-permute-start(bf16[2,512,128]{2,1,0:T(8,128)(2,1)S(1)} %pad_maximum_fusion), channel_id=1, source_target_pairs={{256,0},{264,8},{272,16},{280,24},{288,32},{296,40},{304,48},{312,... | collective-permute-start | bytes 786440 | tf_op jit(solution)/shard_map/ppermute | solution.py:12
  43.6 0.3 copy-done.19
  44.0 0.5 fusion.21
  44.5 0.7 broadcast_in_dim.68
  45.2 4.8 %all-to-all-start.2 = ((f32[8,2,1024]{2,1,0:T(2,128)}), f32[8,2,1024]{2,1,0:T(2,128)S(1)}, u32[]{:S(2)}, u32[]{:S(2)}) async-start(f32[8,2,1024]{2,1,0:T(2,128)} %broadcast_in_dim.68), calls=%async_computation.2 | async-start | bytes 131072 | tf_op jit(solution)/shard_map/all_to_all | solution.py:18
  50.0 4.2 %all-to-all-done.2 = f32[8,2,1024]{2,1,0:T(2,128)S(1)} async-done(((f32[8,2,1024]{2,1,0:T(2,128)}), f32[8,2,1024]{2,1,0:T(2,128)S(1)}, u32[]{:S(2)}, u32[]{:S(2)}) %all-to-all-start.2) | async-done | bytes 65568 | tf_op jit(solution)/shard_map/all_to_all | solution.py:18
  54.5 0.3 copy-done.20
  55.0 4.1 %collective-permute-start = (bf16[1,1280]{1,0:T(2,128)(2,1)S(1)}, bf16[1,1280]{1,0:T(2,128)(2,1)S(1)}, u32[]{:S(2)}, u32[]{:S(2)}) collective-permute-start(bf16[1,1280]{1,0:T(2,128)(2,1)S(1)} %pad_maximum_fusion.1), channel_id=1, source_target_pairs={{256,0},{264,8},{272,16},{280,24},{288,32},{296,40},{304,48},{312,... | collective-permute-start | bytes 7688 | tf_op jit(solution)/shard_map/ppermute | solution.py:12
  59.0 14.0 %collective-permute-done = bf16[1,1280]{1,0:T(2,128)(2,1)S(1)} collective-permute-done((bf16[1,1280]{1,0:T(2,128)(2,1)S(1)}, bf16[1,1280]{1,0:T(2,128)(2,1)S(1)}, u32[]{:S(2)}, u32[]{:S(2)}) %collective-permute-start) | collective-permute-done | bytes 2592 | tf_op jit(solution)/shard_map/ppermute | solution.py:12
  73.2 0.5 copy-done.16
  73.8 0.7 fusion.88
  (103 shorter events, 4.9 us)
Async XLA Ops:
  0.6 43.4 %copy-start = (bf16[512,1024]{1,0:T(8,128)(2,1)S(1)}, bf16[512,1024]{1,0:T(8,128)(2,1)}, u32[]{:S(2)}) copy-start(bf16[512,1024]{1,0:T(8,128)(2,1)} %param.42) | copy-start | bytes 3145732
  0.6 3.4 %copy-start.3 = (bf16[2,512,128]{2,1,0:T(8,128)(2,1)S(1)}, bf16[2,512,128]{2,1,0:T(8,128)(2,1)}, u32[]{:S(2)}) copy-start(bf16[2,512,128]{2,1,0:T(8,128)(2,1)} %param.28) | copy-start | bytes 786436
  4.2 1.5 %copy-start.4 = (bf16[1024,128]{1,0:T(8,128)(2,1)S(1)}, bf16[1024,128]{1,0:T(8,128)(2,1)}, u32[]{:S(2)}) copy-start(bf16[1024,128]{1,0:T(8,128)(2,1)} %param.36) | copy-start | bytes 786436
  4.3 1.4 %copy-start.11 = (bf16[2,1024]{1,0:T(2,128)(2,1)S(1)}, bf16[2,1024]{1,0:T(2,128)(2,1)}, u32[]{:S(2)}) copy-start(bf16[2,1024]{1,0:T(2,128)(2,1)} %param.27) | copy-start | bytes 12292
  4.3 0.7 copy-start.14
  5.0 1.8 %copy-start.2 = (bf16[2,512,128]{2,1,0:T(8,128)(2,1)S(1)}, bf16[2,512,128]{2,1,0:T(8,128)(2,1)}, u32[]{:S(2)}) copy-start(bf16[2,512,128]{2,1,0:T(8,128)(2,1)} %param.29) | copy-start | bytes 786436
  5.7 0.7 copy-start.12
  6.9 1.0 %copy-start.5 = (bf16[1024,128]{1,0:T(8,128)(2,1)S(1)}, bf16[1024,128]{1,0:T(8,128)(2,1)}, u32[]{:S(2)}) copy-start(bf16[1024,128]{1,0:T(8,128)(2,1)} %param.37) | copy-start | bytes 786436
  7.1 1.2 %copy-start.6 = (bf16[128,1024]{1,0:T(8,128)(2,1)S(1)}, bf16[128,1024]{1,0:T(8,128)(2,1)}, u32[]{:S(2)}) copy-start(bf16[128,1024]{1,0:T(8,128)(2,1)} %param.38) | copy-start | bytes 786436
  9.1 13.2 %all-to-all-start = ((f32[8,2,1024]{2,1,0:T(2,128)}), f32[8,2,1024]{2,1,0:T(2,128)S(1)}, u32[]{:S(2)}, u32[]{:S(2)}) async-start(f32[8,2,1024]{2,1,0:T(2,128)} %broadcast_in_dim.40), calls=%async_computation | async-start | bytes 131072 | tf_op jit(solution)/shard_map/all_to_all | solution.py:18
  18.8 0.7 copy-start.15
  18.8 1.9 %copy-start.7 = (bf16[2,512,128]{2,1,0:T(8,128)(2,1)S(1)}, bf16[2,512,128]{2,1,0:T(8,128)(2,1)}, u32[]{:S(2)}) copy-start(bf16[2,512,128]{2,1,0:T(8,128)(2,1)} %param.31) | copy-start | bytes 786436
  20.8 1.0 %copy-start.8 = (bf16[2,512,128]{2,1,0:T(8,128)(2,1)S(1)}, bf16[2,512,128]{2,1,0:T(8,128)(2,1)}, u32[]{:S(2)}) copy-start(bf16[2,512,128]{2,1,0:T(8,128)(2,1)} %param.32) | copy-start | bytes 786436
  21.7 1.4 %copy-start.9 = (bf16[1024,128]{1,0:T(8,128)(2,1)S(1)}, bf16[1024,128]{1,0:T(8,128)(2,1)}, u32[]{:S(2)}) copy-start(bf16[1024,128]{1,0:T(8,128)(2,1)} %param.39) | copy-start | bytes 786436
  22.3 0.7 copy-start.18
  23.1 3.0 %copy-start.10 = (bf16[128,1024]{1,0:T(8,128)(2,1)S(1)}, bf16[128,1024]{1,0:T(8,128)(2,1)}, u32[]{:S(2)}) copy-start(bf16[128,1024]{1,0:T(8,128)(2,1)} %param.40) | copy-start | bytes 786436
  23.4 20.7 %copy-start.1 = (bf16[1024,512]{1,0:T(8,128)(2,1)S(1)}, bf16[1024,512]{1,0:T(8,128)(2,1)}, u32[]{:S(2)}) copy-start(bf16[1024,512]{1,0:T(8,128)(2,1)} %param.41) | copy-start | bytes 3145732
  26.9 16.3 %all-to-all-start.1 = ((f32[8,2,1024]{2,1,0:T(2,128)}), f32[8,2,1024]{2,1,0:T(2,128)S(1)}, u32[]{:S(2)}, u32[]{:S(2)}) async-start(f32[8,2,1024]{2,1,0:T(2,128)} %broadcast_in_dim.41), calls=%async_computation.1 | async-start | bytes 131072 | tf_op jit(solution)/shard_map/all_to_all | solution.py:18
  31.7 42.1 %collective-permute-start.1 = (bf16[2,512,128]{2,1,0:T(8,128)(2,1)S(1)}, bf16[2,512,128]{2,1,0:T(8,128)(2,1)S(1)}, u32[]{:S(2)}, u32[]{:S(2)}) collective-permute-start(bf16[2,512,128]{2,1,0:T(8,128)(2,1)S(1)} %pad_maximum_fusion), channel_id=1, source_target_pairs={{256,0},{264,8},{272,16},{280,24},{288,32},{296,40},{304,48},{312,... | collective-permute-start | bytes 786440 | tf_op jit(solution)/shard_map/ppermute | solution.py:12
  43.3 0.7 copy-start.19
  45.2 9.0 %all-to-all-start.2 = ((f32[8,2,1024]{2,1,0:T(2,128)}), f32[8,2,1024]{2,1,0:T(2,128)S(1)}, u32[]{:S(2)}, u32[]{:S(2)}) async-start(f32[8,2,1024]{2,1,0:T(2,128)} %broadcast_in_dim.68), calls=%async_computation.2 | async-start | bytes 131072 | tf_op jit(solution)/shard_map/all_to_all | solution.py:18
  54.2 0.7 copy-start.20
  55.0 18.1 %collective-permute-start = (bf16[1,1280]{1,0:T(2,128)(2,1)S(1)}, bf16[1,1280]{1,0:T(2,128)(2,1)S(1)}, u32[]{:S(2)}, u32[]{:S(2)}) collective-permute-start(bf16[1,1280]{1,0:T(2,128)(2,1)S(1)} %pad_maximum_fusion.1), channel_id=1, source_target_pairs={{256,0},{264,8},{272,16},{280,24},{288,32},{296,40},{304,48},{312,... | collective-permute-start | bytes 7688 | tf_op jit(solution)/shard_map/ppermute | solution.py:12
  73.1 0.6 copy-start.13
  73.2 0.5 copy-start.16
  73.7 0.7 copy-start.17

commit v4 on v3

--- a/solution.py
+++ b/solution.py
@@ -29,23 +29,15 @@
 def attend(query, keys, values, lengths, fresh_key, fresh_value):
     count, span, width = keys.shape
     heads = width // HEAD_DIM
-    block = min(512, span)
     query_heads = query.reshape(count, heads, HEAD_DIM)
-    steps = (jnp.max(lengths) + block - 1) // block
-    places = lax.iota(jnp.int32, block)
-
-    def score_block(index, board):
-        start = index * block
-        piece = keys.reshape(count, block, heads, HEAD_DIM)
-        scores = jnp.einsum("qhd,qshd->qhs", query_heads, piece, preferred_element_type=jnp.float32)
-        valid = (start + places)[None, None, :] < lengths[:, None, None]
-        scores = jnp.where(valid, scores, -jnp.inf)
-        return scores
-
-    board = lax.fori_loop(
-        0, steps, score_block, jnp.full((count, heads, span), -jnp.inf, jnp.float32)
-    )
-    top = jnp.max(board, axis=2)
+    key_heads = keys.reshape(count, span, heads, HEAD_DIM)
+    value_heads = values.reshape(count, span, heads, HEAD_DIM)
+    scores = jnp.einsum(
+        "qhd,qshd->qhs", query_heads, key_heads, preferred_element_type=jnp.float32
+    )
+    valid = lax.iota(jnp.int32, span)[None, None, :] < lengths[:, None, None]
+    scores = jnp.where(valid, scores, -jnp.inf)
+    top = jnp.max(scores, axis=2)
     if fresh_key is not None:
         own = jnp.sum(
             query_heads.astype(jnp.float32)
@@ -53,17 +45,14 @@
             axis=2,
         )
         top = jnp.maximum(top, own)
-    weights_all = jnp.exp(board - top[:, :, None])
-    total = jnp.sum(weights_all, axis=2)
-
-    def mix_block(index, accum):
-        weights = weights_all.astype(jnp.bfloat16)
-        piece = values.reshape(count, block, heads, HEAD_DIM)
-        return accum + jnp.einsum(
-            "qhs,qshd->qhd", weights, piece, preferred_element_type=jnp.float32
-        )
-
-    mixed = lax.fori_loop(0, steps, mix_block, jnp.zeros((count, heads, HEAD_DIM), jnp.float32))
+    weights = jnp.exp(scores - top[:, :, None])
+    total = jnp.sum(weights, axis=2)
+    mixed = jnp.einsum(
+        "qhs,qshd->qhd",
+        weights.astype(jnp.bfloat16),
+        value_heads,
+        preferred_element_type=jnp.float32,
+    )
     if fresh_key is not None:
         own_weight = jnp.exp(own - top)
         total = total + own_weight
@@ -158,14 +147,11 @@
     )
     chosen = give_slot[0]
     half_axis = lax.axis_size("req") // 2
-    caches = jnp.concatenate((take_slot(self_keys, chosen), take_slot(self_values, chosen)), axis=0)
-    moved = passed_along(caches, "req", half_axis)
-    moved_keys, moved_values = moved[:1], moved[1:]
     layer_out, fresh_keys, fresh_values = decode_layer(
         tokens, self_keys, self_values, self_len, cross_keys, cross_values, cross_len, params
     )
+    count, span, part = self_keys.shape
     width = layer_out.shape[1]
-    part = fresh_keys.shape[1]
     rows = jnp.concatenate(
         (
             take_slot(layer_out, chosen),
@@ -173,11 +159,22 @@
             take_slot(fresh_values, chosen),
         ),
         axis=1,
-    )
-    arrived = passed_along(rows, "req", half_axis)
-    decoded = put_slot(layer_out, arrived[:, :width], chosen)
-    new_keys = put_slot(fresh_keys, arrived[:, width : width + part], chosen)
-    new_values = put_slot(fresh_values, arrived[:, width + part :], chosen)
+    ).reshape(-1, part)
+    parcel = jnp.concatenate(
+        (
+            take_slot(self_keys, chosen).reshape(span, part),
+            take_slot(self_values, chosen).reshape(span, part),
+            rows,
+        ),
+        axis=0,
+    )
+    arrived = passed_along(parcel, "req", half_axis)
+    moved_keys = arrived[:span].reshape(1, span, part)
+    moved_values = arrived[span : 2 * span].reshape(1, span, part)
+    arrived_rows = arrived[2 * span :].reshape(1, -1)
+    decoded = put_slot(layer_out, arrived_rows[:, :width], chosen)
+    new_keys = put_slot(fresh_keys, arrived_rows[:, width : width + part], chosen)
+    new_values = put_slot(fresh_values, arrived_rows[:, width + part :], chosen)
     return (decoded, new_keys, new_values, moved_keys, moved_values)
 
 
@@ -203,7 +200,7 @@
         P(),
         P(),
     )
-    return jax.shard_map(
+    step = jax.shard_map(
         on_device,
         mesh=mesh,
         in_specs=placed,
@@ -216,3 +213,4 @@
         ),
         check_vma=False,
     )
+    return step

time: 75.2 us -> 81.8 us (1.088)
  the two profiles are of different devices: /device:TPU:8 before, /device:TPU:38 now
where the time goes in v4:
time: 81.8 us; the launch traced here: 81.2 us
  waiting for transfers between devices  37.7 us (46%)
  starting transfers between devices  26.1 us (32%)
  local copies, waits for them, and re-layouts  8.83 us (11%)
  matrix products  4.74 us (6%)
  other arithmetic  2.24 us (3%)
  between operations  1.49 us (2%)
    ppermute x1, waiting for transfers between devices, passed_along(): return lax.ppermute(block, axis, route)  23.6 us
    ppermute x1, starting transfers between devices, passed_along(): return lax.ppermute(block, axis, route)  14.8 us
    all_to_all x3, waiting for transfers between devices, head_sum(): gathered = lax.all_to_all(spread, 'head', 0, 0)  14.1 us
    all_to_all x3, starting transfers between devices, head_sum(): gathered = lax.all_to_all(spread, 'head', 0, 0)  11.3 us
    unnamed x46, local copies, waits for them, and re-layouts  5.33 us
    broadcast_in_dim x3, local copies, waits for them, and re-layouts, head_sum(): spread = jnp.broadcast_to(value[None], (count,) + value.shape)  1.96 us
  transfers between devices with their start and end apart: 4, of which 4 were waited for; matrix products, arithmetic and copies ran while one was open for 1% of the time, Pallas kernels for 0%

profile of v4, /device:TPU:38, one launch (start us, length us, event | category | flops | bytes accessed | tf_op | source)
XLA Modules:
  0.0 81.2 jit_solution(10129878351336116600)
XLA Ops:
  0.7 1.2 %fusion.3 = bf16[2,128]{1,0:T(2,128)(2,1)S(1)} fusion(bf16[2,1024]{1,0:T(2,128)(2,1)} %param.19, bf16[1024,128]{1,0:T(8,128)(2,1)} %param.27), kind=kOutput, calls=%fused_computation.5 | convolution fusion | flops 524800 | bytes 266752 | tf_op jit(solution)/shard_map/dot_general | solution.py:82
  2.1 0.8 %convolution_convert_fusion.1 = bf16[2,128]{1,0:T(2,128)(2,1)S(1)} fusion(bf16[2,1024]{1,0:T(2,128)(2,1)} %param.19, bf16[1024,128]{1,0:T(8,128)(2,1)S(1)} %copy-done.4), kind=kOutput, calls=%fused_computation.8 | convolution fusion | flops 524544 | bytes 266752 | tf_op jit(solution)/shard_map/dot_general | solution.py:85
  3.2 0.5 copy-done.18
  4.1 0.2 fusion.9
  4.3 0.4 copy-done.2
  4.8 0.8 copy-done.5
  5.8 0.2 fusion.7
  6.1 0.4 copy-done.6
  6.7 0.7 broadcast_in_dim.26
  7.3 4.6 %all-to-all-start = ((f32[8,2,1024]{2,1,0:T(2,128)}), f32[8,2,1024]{2,1,0:T(2,128)S(1)}, u32[]{:S(2)}, u32[]{:S(2)}) async-start(f32[8,2,1024]{2,1,0:T(2,128)} %broadcast_in_dim.26), calls=%async_computation | async-start | bytes 131072 | tf_op jit(solution)/shard_map/all_to_all | solution.py:18
  12.2 0.8 copy-done.8
  13.0 0.8 %copy.36 = bf16[2,512,128]{1,2,0:T(8,128)(2,1)} copy(bf16[2,512,128]{2,1,0:T(8,128)(2,1)S(1)} %copy-done.8) | data formatting | bytes 524288 | tf_op args[5]
  14.5 3.1 %all-to-all-done = f32[8,2,1024]{2,1,0:T(2,128)S(1)} async-done(((f32[8,2,1024]{2,1,0:T(2,128)}), f32[8,2,1024]{2,1,0:T(2,128)S(1)}, u32[]{:S(2)}, u32[]{:S(2)}) %all-to-all-start) | async-done | bytes 65568 | tf_op jit(solution)/shard_map/all_to_all | solution.py:18
  17.7 0.2 multiply_reduce_fusion.2
  18.0 0.2 fusion.4
  18.6 1.1 %fusion.5 = f32[2,2,1,64]{3,2,1,0:T(1,128)S(1)} fusion(bf16[2,512,2,64]{1,3,2,0:T(8,128)(2,1)} %bitcast.67, bf16[2,2,512,1]{2,1,0,3:T(2,128)(2,1)S(1)} %get-tuple-element.12), kind=kOutput, calls=%fused_computation.16 | convolution fusion | flops 262144 | bytes 267264 | tf_op jit(solution)/shard_map/qhs,qshd->qhd/dot_general | solution.py:50
  19.9 0.2 fusion.94
  20.0 0.7 broadcast_in_dim.28
  20.7 3.4 %all-to-all-start.1 = ((f32[8,2,1024]{2,1,0:T(2,128)}), f32[8,2,1024]{2,1,0:T(2,128)S(1)}, u32[]{:S(2)}, u32[]{:S(2)}) async-start(f32[8,2,1024]{2,1,0:T(2,128)} %broadcast_in_dim.28), calls=%async_computation.1 | async-start | bytes 131072 | tf_op jit(solution)/shard_map/all_to_all | solution.py:18
  24.1 5.5 %all-to-all-done.1 = f32[8,2,1024]{2,1,0:T(2,128)S(1)} async-done(((f32[8,2,1024]{2,1,0:T(2,128)}), f32[8,2,1024]{2,1,0:T(2,128)S(1)}, u32[]{:S(2)}, u32[]{:S(2)}) %all-to-all-start.1) | async-done | bytes 65568 | tf_op jit(solution)/shard_map/all_to_all | solution.py:18
  29.8 0.2 multiply_reduce_fusion.1
  30.0 0.3 copy-done.16
  30.4 0.5 fusion.18
  30.9 0.7 broadcast_in_dim.29
  31.5 3.4 %all-to-all-start.2 = ((f32[8,2,1024]{2,1,0:T(2,128)}), f32[8,2,1024]{2,1,0:T(2,128)S(1)}, u32[]{:S(2)}, u32[]{:S(2)}) async-start(f32[8,2,1024]{2,1,0:T(2,128)} %broadcast_in_dim.29), calls=%async_computation.2 | async-start | bytes 131072 | tf_op jit(solution)/shard_map/all_to_all | solution.py:18
  34.9 5.5 %all-to-all-done.2 = f32[8,2,1024]{2,1,0:T(2,128)S(1)} async-done(((f32[8,2,1024]{2,1,0:T(2,128)}), f32[8,2,1024]{2,1,0:T(2,128)S(1)}, u32[]{:S(2)}, u32[]{:S(2)}) %all-to-all-start.2) | async-done | bytes 65568 | tf_op jit(solution)/shard_map/all_to_all | solution.py:18
  40.6 0.2 multiply_reduce_fusion
  40.8 0.3 copy-done.17
  41.3 14.8 %collective-permute-start = (bf16[1034,128]{1,0:T(8,128)(2,1)S(1)}, bf16[1034,128]{1,0:T(8,128)(2,1)S(1)}, u32[]{:S(2)}, u32[]{:S(2)}) collective-permute-start(bf16[1034,128]{1,0:T(8,128)(2,1)S(1)} %pad_maximum_fusion), channel_id=1, source_target_pairs={{256,0},{264,8},{272,16},{280,24},{288,32},{296,40},{304,48},{312,... | collective-permute-start | bytes 794120 | tf_op jit(solution)/shard_map/ppermute | solution.py:12
  56.1 23.6 %collective-permute-done = bf16[1034,128]{1,0:T(8,128)(2,1)S(1)} collective-permute-done((bf16[1034,128]{1,0:T(8,128)(2,1)S(1)}, bf16[1034,128]{1,0:T(8,128)(2,1)S(1)}, u32[]{:S(2)}, u32[]{:S(2)}) %collective-permute-start) | collective-permute-done | bytes 264736 | tf_op jit(solution)/shard_map/ppermute | solution.py:12
  79.9 0.5 copy-done.13
  80.4 0.7 slice_bitcast_fusion
  (83 shorter events, 3.4 us)
Async XLA Ops:
  0.6 29.7 %copy-start = (bf16[512,1024]{1,0:T(8,128)(2,1)S(1)}, bf16[512,1024]{1,0:T(8,128)(2,1)}, u32[]{:S(2)}) copy-start(bf16[512,1024]{1,0:T(8,128)(2,1)} %param.34) | copy-start | bytes 3145732
  0.6 1.4 %copy-start.4 = (bf16[1024,128]{1,0:T(8,128)(2,1)S(1)}, bf16[1024,128]{1,0:T(8,128)(2,1)}, u32[]{:S(2)}) copy-start(bf16[1024,128]{1,0:T(8,128)(2,1)} %param.28) | copy-start | bytes 786436
  0.7 2.3 %copy-start.3 = (bf16[2,512,128]{2,1,0:T(8,128)(2,1)S(1)}, bf16[2,512,128]{2,1,0:T(8,128)(2,1)}, u32[]{:S(2)}) copy-start(bf16[2,512,128]{2,1,0:T(8,128)(2,1)} %param.20) | copy-start | bytes 786436
  3.0 0.7 copy-start.18
  3.7 0.9 %copy-start.2 = (bf16[2,512,128]{2,1,0:T(8,128)(2,1)S(1)}, bf16[2,512,128]{2,1,0:T(8,128)(2,1)}, u32[]{:S(2)}) copy-start(bf16[2,512,128]{2,1,0:T(8,128)(2,1)} %param.21) | copy-start | bytes 786436
  4.6 0.9 %copy-start.5 = (bf16[1024,128]{1,0:T(8,128)(2,1)S(1)}, bf16[1024,128]{1,0:T(8,128)(2,1)}, u32[]{:S(2)}) copy-start(bf16[1024,128]{1,0:T(8,128)(2,1)} %param.29) | copy-start | bytes 786436
  4.6 1.0 %copy-start.11 = (bf16[2,1024]{1,0:T(2,128)(2,1)S(1)}, bf16[2,1024]{1,0:T(2,128)(2,1)}, u32[]{:S(2)}) copy-start(bf16[2,1024]{1,0:T(2,128)(2,1)} %param.19) | copy-start | bytes 12292
  5.6 1.0 %copy-start.6 = (bf16[128,1024]{1,0:T(8,128)(2,1)S(1)}, bf16[128,1024]{1,0:T(8,128)(2,1)}, u32[]{:S(2)}) copy-start(bf16[128,1024]{1,0:T(8,128)(2,1)} %param.30) | copy-start | bytes 786436
  6.0 6.0 %copy-start.7 = (bf16[2,512,128]{2,1,0:T(8,128)(2,1)S(1)}, bf16[2,512,128]{2,1,0:T(8,128)(2,1)}, u32[]{:S(2)}) copy-start(bf16[2,512,128]{2,1,0:T(8,128)(2,1)} %param.23) | copy-start | bytes 786436
  7.3 4.6 %copy-start.19 = (s32[2]{0:T(128)S(1)}, s32[2]{0:T(128)}, u32[]{:S(2)}) copy-start(s32[2]{0:T(128)} %param.25) | copy-start | bytes 28
  7.3 10.2 %all-to-all-start = ((f32[8,2,1024]{2,1,0:T(2,128)}), f32[8,2,1024]{2,1,0:T(2,128)S(1)}, u32[]{:S(2)}, u32[]{:S(2)}) async-start(f32[8,2,1024]{2,1,0:T(2,128)} %broadcast_in_dim.26), calls=%async_computation | async-start | bytes 131072 | tf_op jit(solution)/shard_map/all_to_all | solution.py:18
  12.0 1.0 %copy-start.8 = (bf16[2,512,128]{2,1,0:T(8,128)(2,1)S(1)}, bf16[2,512,128]{2,1,0:T(8,128)(2,1)}, u32[]{:S(2)}) copy-start(bf16[2,512,128]{2,1,0:T(8,128)(2,1)} %param.24) | copy-start | bytes 786436
  13.0 5.0 %copy-start.15 = (f32[1024]{0:T(1024)S(1)}, f32[1024]{0:T(1024)}, u32[]{:S(2)}) copy-start(f32[1024]{0:T(1024)} %param.35) | copy-start | bytes 12292
  13.0 5.1 %copy-start.9 = (bf16[1024,128]{1,0:T(8,128)(2,1)S(1)}, bf16[1024,128]{1,0:T(8,128)(2,1)}, u32[]{:S(2)}) copy-start(bf16[1024,128]{1,0:T(8,128)(2,1)} %param.31) | copy-start | bytes 786436
  17.5 2.3 %copy-start.10 = (bf16[128,1024]{1,0:T(8,128)(2,1)S(1)}, bf16[128,1024]{1,0:T(8,128)(2,1)}, u32[]{:S(2)}) copy-start(bf16[128,1024]{1,0:T(8,128)(2,1)} %param.32) | copy-start | bytes 786436
  17.6 12.8 %copy-start.1 = (bf16[1024,512]{1,0:T(8,128)(2,1)S(1)}, bf16[1024,512]{1,0:T(8,128)(2,1)}, u32[]{:S(2)}) copy-start(bf16[1024,512]{1,0:T(8,128)(2,1)} %param.33) | copy-start | bytes 3145732
  20.7 8.9 %all-to-all-start.1 = ((f32[8,2,1024]{2,1,0:T(2,128)}), f32[8,2,1024]{2,1,0:T(2,128)S(1)}, u32[]{:S(2)}, u32[]{:S(2)}) async-start(f32[8,2,1024]{2,1,0:T(2,128)} %broadcast_in_dim.28), calls=%async_computation.1 | async-start | bytes 131072 | tf_op jit(solution)/shard_map/all_to_all | solution.py:18
  29.6 0.7 copy-start.16
  31.5 8.9 %all-to-all-start.2 = ((f32[8,2,1024]{2,1,0:T(2,128)}), f32[8,2,1024]{2,1,0:T(2,128)S(1)}, u32[]{:S(2)}, u32[]{:S(2)}) async-start(f32[8,2,1024]{2,1,0:T(2,128)} %broadcast_in_dim.29), calls=%async_computation.2 | async-start | bytes 131072 | tf_op jit(solution)/shard_map/all_to_all | solution.py:18
  40.4 0.7 copy-start.17
  41.3 38.5 %collective-permute-start = (bf16[1034,128]{1,0:T(8,128)(2,1)S(1)}, bf16[1034,128]{1,0:T(8,128)(2,1)S(1)}, u32[]{:S(2)}, u32[]{:S(2)}) collective-permute-start(bf16[1034,128]{1,0:T(8,128)(2,1)S(1)} %pad_maximum_fusion), channel_id=1, source_target_pairs={{256,0},{264,8},{272,16},{280,24},{288,32},{296,40},{304,48},{312,... | collective-permute-start | bytes 794120 | tf_op jit(solution)/shard_map/ppermute | solution.py:12
  79.8 1.4 %copy-start.12 = (bf16[2,1024]{1,0:T(2,128)(2,1)}, bf16[2,1024]{1,0:T(2,128)(2,1)S(1)}, u32[]{:S(2)}) copy-start(bf16[2,1024]{1,0:T(2,128)(2,1)S(1)} %dynamic_update_slice.9) | copy-start | bytes 12292
  79.9 0.5 copy-start.13
  80.4 0.8 copy-start.14

commit v5 on v4

--- a/solution.py
+++ b/solution.py
@@ -4,12 +4,6 @@
 from jax.sharding import PartitionSpec as P
 
 HEAD_DIM = 64
-
-
-def passed_along(block, axis, distance):
-    devices = range(lax.axis_size(axis))
-    route = [((i - distance) % len(devices), i) for i in devices]
-    return lax.ppermute(block, axis, route)
 
 
 def head_sum(value):
@@ -76,7 +70,7 @@
         w_down,
         gain_self,
         gain_cross,
-        gain_final,
+        _,
     ) = params
     scale = HEAD_DIM ** (-0.5)
     query = (jnp.dot(tokens, w_query, preferred_element_type=jnp.float32) * scale).astype(
@@ -98,9 +92,8 @@
     hidden = jax.nn.gelu(
         jnp.dot(second, w_up, preferred_element_type=jnp.float32), approximate=False
     ).astype(jnp.bfloat16)
-    ffn_total = head_sum(jnp.dot(hidden, w_down, preferred_element_type=jnp.float32))
-    layer_out = layer_norm(second.astype(jnp.float32) + ffn_total, gain_final).astype(jnp.bfloat16)
-    return (layer_out, fresh_keys, fresh_values)
+    ffn_part = jnp.dot(hidden, w_down, preferred_element_type=jnp.float32)
+    return (second, ffn_part, fresh_keys, fresh_values)
 
 
 def take_slot(array, chosen):
@@ -146,48 +139,63 @@
         gain_final,
     )
     chosen = give_slot[0]
-    half_axis = lax.axis_size("req") // 2
-    layer_out, fresh_keys, fresh_values = decode_layer(
+    kept = 1 - chosen
+    flip = [(0, 1), (1, 0)]
+    heads = lax.axis_size("head")
+    second, ffn_part, fresh_keys, fresh_values = decode_layer(
         tokens, self_keys, self_values, self_len, cross_keys, cross_values, cross_len, params
     )
-    count, span, part = self_keys.shape
-    width = layer_out.shape[1]
-    rows = jnp.concatenate(
-        (
-            take_slot(layer_out, chosen),
-            take_slot(fresh_keys, chosen),
-            take_slot(fresh_values, chosen),
-        ),
-        axis=1,
-    ).reshape(-1, part)
+    _, span, part = self_keys.shape
     parcel = jnp.concatenate(
         (
             take_slot(self_keys, chosen).reshape(span, part),
             take_slot(self_values, chosen).reshape(span, part),
-            rows,
+            take_slot(fresh_keys, chosen),
+            take_slot(fresh_values, chosen),
         ),
         axis=0,
     )
-    arrived = passed_along(parcel, "req", half_axis)
+    arrived = lax.ppermute(parcel, "zh", flip)
+    partner_second = lax.ppermute(take_slot(second, chosen), "zh", flip)
     moved_keys = arrived[:span].reshape(1, span, part)
     moved_values = arrived[span : 2 * span].reshape(1, span, part)
-    arrived_rows = arrived[2 * span :].reshape(1, -1)
-    decoded = put_slot(layer_out, arrived_rows[:, :width], chosen)
-    new_keys = put_slot(fresh_keys, arrived_rows[:, width : width + part], chosen)
-    new_values = put_slot(fresh_values, arrived_rows[:, width + part :], chosen)
+    new_keys = put_slot(fresh_keys, arrived[2 * span : 2 * span + 1], chosen)
+    new_values = put_slot(fresh_values, arrived[2 * span + 1 :], chosen)
+    side = lax.axis_index("zh")
+    mine = (lax.iota(jnp.int32, 2) == side)[:, None, None, None]
+    chunks = jnp.where(
+        mine, take_slot(ffn_part, kept)[None, None], take_slot(ffn_part, chosen)[None, None]
+    )
+    chunks = jnp.broadcast_to(chunks, (2, heads) + chunks.shape[2:])
+    chunks = chunks.reshape((2 * heads,) + chunks.shape[2:])
+    gathered = lax.all_to_all(chunks, ("zh", "head"), 0, 0)
+    gathered = gathered.reshape((2, heads) + gathered.shape[1:])
+    own_sum = jnp.sum(lax.dynamic_index_in_dim(gathered, side, 0, keepdims=False), axis=0)
+    far_sum = jnp.sum(lax.dynamic_index_in_dim(gathered, 1 - side, 0, keepdims=False), axis=0)
+    own_out = layer_norm(take_slot(second, kept).astype(jnp.float32) + own_sum, gain_final)
+    far_out = layer_norm(partner_second.astype(jnp.float32) + far_sum, gain_final)
+    decoded = put_slot(
+        put_slot(second, own_out.astype(jnp.bfloat16), kept),
+        far_out.astype(jnp.bfloat16),
+        chosen,
+    )
     return (decoded, new_keys, new_values, moved_keys, moved_values)
 
 
 def solution(mesh):
+    req = mesh.shape["req"]
+    split = jax.sharding.Mesh(
+        mesh.devices.reshape(2, req // 2, mesh.shape["head"]), ("zh", "zl", "head")
+    )
     placed = (
-        P("req", None),
-        P("req", None, "head"),
-        P("req", None, "head"),
-        P("req"),
-        P("req", None, "head"),
-        P("req", None, "head"),
-        P("req"),
-        P("req"),
+        P(("zh", "zl"), None),
+        P(("zh", "zl"), None, "head"),
+        P(("zh", "zl"), None, "head"),
+        P(("zh", "zl")),
+        P(("zh", "zl"), None, "head"),
+        P(("zh", "zl"), None, "head"),
+        P(("zh", "zl")),
+        P(("zh", "zl")),
         P(None, "head"),
         P(None, "head"),
         P(None, "head"),
@@ -200,17 +208,16 @@
         P(),
         P(),
     )
-    step = jax.shard_map(
+    return jax.shard_map(
         on_device,
-        mesh=mesh,
+        mesh=split,
         in_specs=placed,
         out_specs=(
-            P("req", None),
-            P("req", "head"),
-            P("req", "head"),
-            P("req", None, "head"),
-            P("req", None, "head"),
+            P(("zh", "zl"), None),
+            P(("zh", "zl"), "head"),
+            P(("zh", "zl"), "head"),
+            P(("zh", "zl"), None, "head"),
+            P(("zh", "zl"), None, "head"),
         ),
         check_vma=False,
     )
-    return step

time: 81.8 us -> 71.9 us (0.88)
  the two profiles are of different devices: /device:TPU:38 before, /device:TPU:1 now
where the time goes in v5:
time: 71.9 us; the launch traced here: 71.3 us
  starting transfers between devices  42.6 us (59%)
  local copies, waits for them, and re-layouts  9.26 us (13%)
  waiting for transfers between devices  6.15 us (9%)
  matrix products  4.74 us (7%)
  other arithmetic  4.33 us (6%)
  between operations  4.24 us (6%)
    all_to_all x2, starting transfers between devices, head_sum(): gathered = lax.all_to_all(spread, 'head', 0, 0)  15.2 us
    ppermute x1, starting transfers between devices, on_device(): partner_second = lax.ppermute(take_slot(second, chosen), 'zh', flip)  12 us
    ppermute x1, starting transfers between devices, on_device(): arrived = lax.ppermute(parcel, 'zh', flip)  11.3 us
    unnamed x44, local copies, waits for them, and re-layouts  5.57 us
    all_to_all x2, waiting for transfers between devices, head_sum(): gathered = lax.all_to_all(spread, 'head', 0, 0)  4.85 us
    all_to_all x1, starting transfers between devices, on_device(): gathered = lax.all_to_all(chunks, ('zh', 'head'), 0, 0)  4.06 us
    reduce_sum x4, other arithmetic, layer_norm(): spread = jnp.mean(centred * centred, axis=-1, keepdims=True)  1.6 us
    reduce_sum x4, other arithmetic, layer_norm(): mean = jnp.mean(value, axis=-1, keepdims=True)  1.47 us
  transfers between devices with their start and end apart: 5, of which 2 were waited for; matrix products, arithmetic and copies ran while one was open for 11% of the time, Pallas kernels for 0%

profile of v5, /device:TPU:1, one launch (start us, length us, event | category | flops | bytes accessed | tf_op | source)
XLA Modules:
  0.0 71.3 jit_solution(16460220684633142745)
XLA Ops:
  0.7 1.2 %fusion.3 = bf16[2,128]{1,0:T(2,128)(2,1)S(1)} fusion(bf16[2,1024]{1,0:T(2,128)(2,1)} %param.19, bf16[1024,128]{1,0:T(8,128)(2,1)} %param.27), kind=kOutput, calls=%fused_computation.5 | convolution fusion | flops 524800 | bytes 266752 | tf_op jit(solution)/shard_map/dot_general | solution.py:76
  2.1 0.8 %convolution_convert_fusion.1 = bf16[2,128]{1,0:T(2,128)(2,1)S(1)} fusion(bf16[2,1024]{1,0:T(2,128)(2,1)} %param.19, bf16[1024,128]{1,0:T(8,128)(2,1)S(1)} %copy-done.4), kind=kOutput, calls=%fused_computation.8 | convolution fusion | flops 524544 | bytes 266752 | tf_op jit(solution)/shard_map/dot_general | solution.py:79
  3.2 0.5 copy-done.18
  4.1 0.2 fusion.9
  4.3 0.4 copy-done.2
  4.8 0.8 %copy-done.5 = bf16[1024,128]{1,0:T(8,128)(2,1)S(1)} copy-done((bf16[1024,128]{1,0:T(8,128)(2,1)S(1)}, bf16[1024,128]{1,0:T(8,128)(2,1)}, u32[]{:S(2)}) %copy-start.5) | copy-done | bytes 262168
  5.8 0.2 fusion.7
  6.1 0.4 copy-done.6
  6.7 0.7 broadcast_in_dim.58
  7.3 10.1 %all-to-all-start = ((f32[8,2,1024]{2,1,0:T(2,128)}), f32[8,2,1024]{2,1,0:T(2,128)S(1)}, u32[]{:S(2)}, u32[]{:S(2)}) async-start(f32[8,2,1024]{2,1,0:T(2,128)} %broadcast_in_dim.58), calls=%async_computation | async-start | bytes 131072 | tf_op jit(solution)/shard_map/all_to_all | solution.py:12
  18.2 11.3 %collective-permute-start.1 = (bf16[1026,128]{1,0:T(8,128)(2,1)S(1)}, bf16[1026,128]{1,0:T(8,128)(2,1)S(1)}, u32[]{:S(2)}, u32[]{:S(2)}) collective-permute-start(bf16[1026,128]{1,0:T(8,128)(2,1)S(1)} %concatenate.3), channel_id=1, source_target_pairs={{0,256},{256,0},{1,257},{257,1},{2,258},{258,2},{3,259},{259,3},{4... | collective-permute-start | bytes 787976 | tf_op jit(solution)/shard_map/ppermute | solution.py:158
  29.8 0.8 %copy-done.8 = bf16[2,512,128]{2,1,0:T(8,128)(2,1)S(1)} copy-done((bf16[2,512,128]{2,1,0:T(8,128)(2,1)S(1)}, bf16[2,512,128]{2,1,0:T(8,128)(2,1)}, u32[]{:S(2)}) %copy-start.8) | copy-done | bytes 262168
  30.6 0.8 %copy.40 = bf16[2,512,128]{1,2,0:T(8,128)(2,1)} copy(bf16[2,512,128]{2,1,0:T(8,128)(2,1)S(1)} %copy-done.8) | data formatting | bytes 524288 | tf_op args[5]
  31.6 0.2 multiply_reduce_fusion.1
  32.5 1.1 %fusion.5 = f32[2,2,1,64]{3,2,1,0:T(1,128)S(1)} fusion(bf16[2,512,2,64]{1,3,2,0:T(8,128)(2,1)} %bitcast.68, bf16[2,2,512,1]{2,1,0,3:T(2,128)(2,1)S(1)} %get-tuple-element.20), kind=kOutput, calls=%fused_computation.17 | convolution fusion | flops 262144 | bytes 267264 | tf_op jit(solution)/shard_map/qhs,qshd->qhd/dot_general | solution.py:44
  33.9 0.7 broadcast_in_dim.60
  34.6 5.1 %all-to-all-start.1 = ((f32[8,2,1024]{2,1,0:T(2,128)}), f32[8,2,1024]{2,1,0:T(2,128)S(1)}, u32[]{:S(2)}, u32[]{:S(2)}) async-start(f32[8,2,1024]{2,1,0:T(2,128)} %broadcast_in_dim.60), calls=%async_computation.1 | async-start | bytes 131072 | tf_op jit(solution)/shard_map/all_to_all | solution.py:12
  39.7 4.8 %all-to-all-done.1 = f32[8,2,1024]{2,1,0:T(2,128)S(1)} async-done(((f32[8,2,1024]{2,1,0:T(2,128)}), f32[8,2,1024]{2,1,0:T(2,128)S(1)}, u32[]{:S(2)}, u32[]{:S(2)}) %all-to-all-start.1) | async-done | bytes 65568 | tf_op jit(solution)/shard_map/all_to_all | solution.py:12
  44.7 0.2 multiply_reduce_fusion
  44.9 0.3 copy-done.16
  45.3 0.5 fusion.18
  45.9 0.7 broadcast_in_dim.102
  46.6 4.1 %all-to-all-start.2 = ((f32[16,1,1024]{2,1,0:T(1,128)}), f32[16,1,1024]{2,1,0:T(1,128)S(1)}, u32[]{:S(2)}, u32[]{:S(2)}) async-start(f32[16,1,1024]{2,1,0:T(1,128)} %broadcast_in_dim.102), calls=%async_computation.2 | async-start | bytes 131072 | tf_op jit(solution)/shard_map/all_to_all | solution.py:171
  50.6 12.0 %collective-permute-start = (bf16[1,1024]{1,0:T(2,128)(2,1)S(1)}, bf16[1,1024]{1,0:T(2,128)(2,1)S(1)}, u32[]{:S(2)}, u32[]{:S(2)}) collective-permute-start(bf16[1,1024]{1,0:T(2,128)(2,1)S(1)} %constant_dynamic-slice_fusion.2), channel_id=1, source_target_pairs={{0,256},{256,0},{1,257},{257,1},{2,258},{258,2},{3,259},{259,3},{4... | collective-permute-start | bytes 6152 | tf_op jit(solution)/shard_map/ppermute | solution.py:159
  62.8 0.5 copy-done.13
  63.3 0.7 %slice_bitcast_fusion = (bf16[1,512,128]{2,1,0:T(8,128)(2,1)}, bf16[1,512,128]{2,1,0:T(8,128)(2,1)}) fusion(bf16[1026,128]{1,0:T(8,128)(2,1)S(1)} %collective-permute-done.1), kind=kLoop, calls=%fused_computation.9 | loop fusion | bytes 524288 | tf_op jit(solution)/shard_map/reshape | solution.py:161
  64.0 1.3 %all-to-all-done.2 = f32[16,1,1024]{2,1,0:T(1,128)S(1)} async-done(((f32[16,1,1024]{2,1,0:T(1,128)}), f32[16,1,1024]{2,1,0:T(1,128)S(1)}, u32[]{:S(2)}, u32[]{:S(2)}) %all-to-all-start.2) | async-done | bytes 65568 | tf_op jit(solution)/shard_map/all_to_all | solution.py:171
  65.4 0.6 fusion.87
  66.7 0.6 multiply_reduce_fusion.3
  68.0 0.6 fusion.86
  69.2 0.6 multiply_reduce_fusion.2
  70.7 0.6 copy-done.12
  (86 shorter events, 3.7 us)
Async XLA Ops:
  0.6 44.6 %copy-start = (bf16[512,1024]{1,0:T(8,128)(2,1)S(1)}, bf16[512,1024]{1,0:T(8,128)(2,1)}, u32[]{:S(2)}) copy-start(bf16[512,1024]{1,0:T(8,128)(2,1)} %param.34) | copy-start | bytes 3145732
  0.6 1.4 %copy-start.4 = (bf16[1024,128]{1,0:T(8,128)(2,1)S(1)}, bf16[1024,128]{1,0:T(8,128)(2,1)}, u32[]{:S(2)}) copy-start(bf16[1024,128]{1,0:T(8,128)(2,1)} %param.28) | copy-start | bytes 786436
  0.7 2.3 %copy-start.3 = (bf16[2,512,128]{2,1,0:T(8,128)(2,1)S(1)}, bf16[2,512,128]{2,1,0:T(8,128)(2,1)}, u32[]{:S(2)}) copy-start(bf16[2,512,128]{2,1,0:T(8,128)(2,1)} %param.20) | copy-start | bytes 786436
  3.0 0.7 copy-start.18
  3.7 0.9 %copy-start.2 = (bf16[2,512,128]{2,1,0:T(8,128)(2,1)S(1)}, bf16[2,512,128]{2,1,0:T(8,128)(2,1)}, u32[]{:S(2)}) copy-start(bf16[2,512,128]{2,1,0:T(8,128)(2,1)} %param.21) | copy-start | bytes 786436
  4.6 0.9 %copy-start.5 = (bf16[1024,128]{1,0:T(8,128)(2,1)S(1)}, bf16[1024,128]{1,0:T(8,128)(2,1)}, u32[]{:S(2)}) copy-start(bf16[1024,128]{1,0:T(8,128)(2,1)} %param.29) | copy-start | bytes 786436
  4.6 1.0 %copy-start.11 = (bf16[2,1024]{1,0:T(2,128)(2,1)S(1)}, bf16[2,1024]{1,0:T(2,128)(2,1)}, u32[]{:S(2)}) copy-start(bf16[2,1024]{1,0:T(2,128)(2,1)} %param.19) | copy-start | bytes 12292
  5.6 1.0 %copy-start.6 = (bf16[128,1024]{1,0:T(8,128)(2,1)S(1)}, bf16[128,1024]{1,0:T(8,128)(2,1)}, u32[]{:S(2)}) copy-start(bf16[128,1024]{1,0:T(8,128)(2,1)} %param.30) | copy-start | bytes 786436
  7.3 24.1 %all-to-all-start = ((f32[8,2,1024]{2,1,0:T(2,128)}), f32[8,2,1024]{2,1,0:T(2,128)S(1)}, u32[]{:S(2)}, u32[]{:S(2)}) async-start(f32[8,2,1024]{2,1,0:T(2,128)} %broadcast_in_dim.58), calls=%async_computation | async-start | bytes 131072 | tf_op jit(solution)/shard_map/all_to_all | solution.py:12
  18.1 11.4 %copy-start.19 = (s32[2]{0:T(128)S(1)}, s32[2]{0:T(128)}, u32[]{:S(2)}) copy-start(s32[2]{0:T(128)} %param.25) | copy-start | bytes 28
  18.1 11.5 %copy-start.7 = (bf16[2,512,128]{2,1,0:T(8,128)(2,1)S(1)}, bf16[2,512,128]{2,1,0:T(8,128)(2,1)}, u32[]{:S(2)}) copy-start(bf16[2,512,128]{2,1,0:T(8,128)(2,1)} %param.23) | copy-start | bytes 786436
  18.2 44.5 %collective-permute-start.1 = (bf16[1026,128]{1,0:T(8,128)(2,1)S(1)}, bf16[1026,128]{1,0:T(8,128)(2,1)S(1)}, u32[]{:S(2)}, u32[]{:S(2)}) collective-permute-start(bf16[1026,128]{1,0:T(8,128)(2,1)S(1)} %concatenate.3), channel_id=1, source_target_pairs={{0,256},{256,0},{1,257},{257,1},{2,258},{258,2},{3,259},{259,3},{4... | collective-permute-start | bytes 787976 | tf_op jit(solution)/shard_map/ppermute | solution.py:158
  29.6 1.0 %copy-start.8 = (bf16[2,512,128]{2,1,0:T(8,128)(2,1)S(1)}, bf16[2,512,128]{2,1,0:T(8,128)(2,1)}, u32[]{:S(2)}) copy-start(bf16[2,512,128]{2,1,0:T(8,128)(2,1)} %param.24) | copy-start | bytes 786436
  29.6 2.2 %copy-start.15 = (f32[1024]{0:T(1024)S(1)}, f32[1024]{0:T(1024)}, u32[]{:S(2)}) copy-start(f32[1024]{0:T(1024)} %param.35) | copy-start | bytes 12292
  29.6 2.2 %copy-start.9 = (bf16[1024,128]{1,0:T(8,128)(2,1)S(1)}, bf16[1024,128]{1,0:T(8,128)(2,1)}, u32[]{:S(2)}) copy-start(bf16[1024,128]{1,0:T(8,128)(2,1)} %param.31) | copy-start | bytes 786436
  30.6 14.7 %copy-start.1 = (bf16[1024,512]{1,0:T(8,128)(2,1)S(1)}, bf16[1024,512]{1,0:T(8,128)(2,1)}, u32[]{:S(2)}) copy-start(bf16[1024,512]{1,0:T(8,128)(2,1)} %param.33) | copy-start | bytes 3145732
  32.1 1.6 %copy-start.10 = (bf16[128,1024]{1,0:T(8,128)(2,1)S(1)}, bf16[128,1024]{1,0:T(8,128)(2,1)}, u32[]{:S(2)}) copy-start(bf16[128,1024]{1,0:T(8,128)(2,1)} %param.32) | copy-start | bytes 786436
  34.6 9.9 %all-to-all-start.1 = ((f32[8,2,1024]{2,1,0:T(2,128)}), f32[8,2,1024]{2,1,0:T(2,128)S(1)}, u32[]{:S(2)}, u32[]{:S(2)}) async-start(f32[8,2,1024]{2,1,0:T(2,128)} %broadcast_in_dim.60), calls=%async_computation.1 | async-start | bytes 131072 | tf_op jit(solution)/shard_map/all_to_all | solution.py:12
  44.5 0.7 copy-start.16
  46.6 18.8 %all-to-all-start.2 = ((f32[16,1,1024]{2,1,0:T(1,128)}), f32[16,1,1024]{2,1,0:T(1,128)S(1)}, u32[]{:S(2)}, u32[]{:S(2)}) async-start(f32[16,1,1024]{2,1,0:T(1,128)} %broadcast_in_dim.102), calls=%async_computation.2 | async-start | bytes 131072 | tf_op jit(solution)/shard_map/all_to_all | solution.py:171
  50.6 17.3 %collective-permute-start = (bf16[1,1024]{1,0:T(2,128)(2,1)S(1)}, bf16[1,1024]{1,0:T(2,128)(2,1)S(1)}, u32[]{:S(2)}, u32[]{:S(2)}) collective-permute-start(bf16[1,1024]{1,0:T(2,128)(2,1)S(1)} %constant_dynamic-slice_fusion.2), channel_id=1, source_target_pairs={{0,256},{256,0},{1,257},{257,1},{2,258},{258,2},{3,259},{259,3},{4... | collective-permute-start | bytes 6152 | tf_op jit(solution)/shard_map/ppermute | solution.py:159
  62.7 0.5 copy-start.13
  63.3 0.8 %copy-start.14 = (bf16[2,128]{1,0:T(2,128)(2,1)}, bf16[2,128]{1,0:T(2,128)(2,1)S(1)}, u32[]{:S(2)}) copy-start(bf16[2,128]{1,0:T(2,128)(2,1)S(1)} %dynamic_update_slice.15) | copy-start | bytes 1540
  69.8 0.7 copy-start.17
  70.7 0.6 copy-start.12

commit v6 on v3

--- a/solution.py
+++ b/solution.py
@@ -29,48 +29,38 @@
 def attend(query, keys, values, lengths, fresh_key, fresh_value):
     count, span, width = keys.shape
     heads = width // HEAD_DIM
-    block = min(512, span)
-    query_heads = query.reshape(count, heads, HEAD_DIM)
-    steps = (jnp.max(lengths) + block - 1) // block
-    places = lax.iota(jnp.int32, block)
-
-    def score_block(index, board):
-        start = index * block
-        piece = keys.reshape(count, block, heads, HEAD_DIM)
-        scores = jnp.einsum("qhd,qshd->qhs", query_heads, piece, preferred_element_type=jnp.float32)
-        valid = (start + places)[None, None, :] < lengths[:, None, None]
-        scores = jnp.where(valid, scores, -jnp.inf)
-        return scores
-
-    board = lax.fori_loop(
-        0, steps, score_block, jnp.full((count, heads, span), -jnp.inf, jnp.float32)
-    )
-    top = jnp.max(board, axis=2)
+    owner = lax.iota(jnp.int32, width) // HEAD_DIM
+    pick = owner[:, None] == lax.iota(jnp.int32, heads)[None, :]
+    query_blocks = jnp.where(pick[None], query[:, :, None], jnp.zeros((), query.dtype))
+    scores = jnp.einsum(
+        "qsd,qdh->qsh", keys, query_blocks, preferred_element_type=jnp.float32
+    )
+    valid = lax.iota(jnp.int32, span)[None, :, None] < lengths[:, None, None]
+    scores = jnp.where(valid, scores, -jnp.inf)
+    top = jnp.max(scores, axis=1)
     if fresh_key is not None:
         own = jnp.sum(
-            query_heads.astype(jnp.float32)
+            query.reshape(count, heads, HEAD_DIM).astype(jnp.float32)
             * fresh_key.reshape(count, heads, HEAD_DIM).astype(jnp.float32),
             axis=2,
         )
         top = jnp.maximum(top, own)
-    weights_all = jnp.exp(board - top[:, :, None])
-    total = jnp.sum(weights_all, axis=2)
-
-    def mix_block(index, accum):
-        weights = weights_all.astype(jnp.bfloat16)
-        piece = values.reshape(count, block, heads, HEAD_DIM)
-        return accum + jnp.einsum(
-            "qhs,qshd->qhd", weights, piece, preferred_element_type=jnp.float32
-        )
-
-    mixed = lax.fori_loop(0, steps, mix_block, jnp.zeros((count, heads, HEAD_DIM), jnp.float32))
+    weights = jnp.exp(scores - top[:, None, :])
+    total = jnp.sum(weights, axis=1)
+    mixed_all = jnp.einsum(
+        "qsh,qsd->qhd",
+        weights.astype(jnp.bfloat16),
+        values,
+        preferred_element_type=jnp.float32,
+    )
+    mixed = jnp.sum(jnp.where(pick.T[None], mixed_all, 0.0), axis=1)
     if fresh_key is not None:
         own_weight = jnp.exp(own - top)
         total = total + own_weight
-        mixed = mixed + own_weight.astype(jnp.bfloat16).astype(jnp.float32)[
-            :, :, None
-        ] * fresh_value.reshape(count, heads, HEAD_DIM).astype(jnp.float32)
-    return (mixed / total[:, :, None]).astype(jnp.bfloat16).reshape(count, width)
+        mixed = mixed + jnp.repeat(
+            own_weight.astype(jnp.bfloat16).astype(jnp.float32), HEAD_DIM, axis=1
+        ) * fresh_value.astype(jnp.float32)
+    return (mixed / jnp.repeat(total, HEAD_DIM, axis=1)).astype(jnp.bfloat16)
 
 
 def decode_layer(

time: 75.2 us -> 68 us (0.904)
  the two profiles are of different devices: /device:TPU:8 before, /device:TPU:1 now
where the time goes in v6:
time: 68 us; the launch traced here: 67.1 us
  starting transfers between devices  33.4 us (49%)
  waiting for transfers between devices  20 us (29%)
  local copies, waits for them, and re-layouts  5.77 us (8%)
  matrix products  4.3 us (6%)
  other arithmetic  1.98 us (3%)
  between operations  1.55 us (2%)
    all_to_all x3, starting transfers between devices, head_sum(): gathered = lax.all_to_all(spread, 'head', 0, 0)  19.2 us
    ppermute x2, starting transfers between devices, passed_along(): return lax.ppermute(block, axis, route)  14.2 us
    ppermute x2, waiting for transfers between devices, passed_along(): return lax.ppermute(block, axis, route)  10.3 us
    all_to_all x3, waiting for transfers between devices, head_sum(): gathered = lax.all_to_all(spread, 'head', 0, 0)  9.71 us
    unnamed x38, local copies, waits for them, and re-layouts  2.35 us
    broadcast_in_dim x3, local copies, waits for them, and re-layouts, head_sum(): spread = jnp.broadcast_to(value[None], (count,) + value.shape)  1.96 us
    dot_general x2, matrix products, attend(): jnp.einsum('qsh,qsd->qhd', weights.astype(jnp.bfloat16), values, preferre...  1.4 us
  transfers between devices with their start and end apart: 5, of which 3 were waited for; matrix products, arithmetic and copies ran while one was open for 8% of the time, Pallas kernels for 0%

profile of v6, /device:TPU:1, one launch (start us, length us, event | category | flops | bytes accessed | tf_op | source)
XLA Modules:
  0.0 67.1 jit_solution(1749271500596621688)
XLA Ops:
  0.7 0.7 %copy-done.9 = bf16[2,1024]{1,0:T(2,128)(2,1)S(1)} copy-done((bf16[2,1024]{1,0:T(2,128)(2,1)S(1)}, bf16[2,1024]{1,0:T(2,128)(2,1)}, u32[]{:S(2)}) %copy-start.9) | copy-done | bytes 4120
  1.4 1.1 %convolution_convert_fusion = bf16[2,128]{1,0:T(2,128)(2,1)S(1)} fusion(bf16[2,1024]{1,0:T(2,128)(2,1)S(1)} %copy-done.9, bf16[1024,128]{1,0:T(8,128)(2,1)} %param.29), kind=kOutput, calls=%fused_computation.12 | convolution fusion | flops 524544 | bytes 266752 | tf_op jit(solution)/shard_map/dot_general | solution.py:87
  2.6 0.2 fusion.4
  2.7 0.2 convert_multiply_fusion
  3.0 0.2 copy-done.17
  3.5 0.3 fusion.97
  4.0 0.2 fusion.6
  4.3 0.2 fusion.2
  4.6 0.1 fusion.53
  4.7 0.7 broadcast_in_dim.128
  5.4 10.1 %all-to-all-start = ((f32[8,2,1024]{2,1,0:T(2,128)}), f32[8,2,1024]{2,1,0:T(2,128)S(1)}, u32[]{:S(2)}, u32[]{:S(2)}) async-start(f32[8,2,1024]{2,1,0:T(2,128)} %broadcast_in_dim.128), calls=%async_computation | async-start | bytes 131072 | tf_op jit(solution)/shard_map/all_to_all | solution.py:18
  16.3 11.4 %collective-permute-start.1 = (bf16[2,512,128]{2,1,0:T(8,128)(2,1)S(1)}, bf16[2,512,128]{2,1,0:T(8,128)(2,1)S(1)}, u32[]{:S(2)}, u32[]{:S(2)}) collective-permute-start(bf16[2,512,128]{2,1,0:T(8,128)(2,1)S(1)} %pad_maximum_fusion), channel_id=1, source_target_pairs={{256,0},{264,8},{272,16},{280,24},{288,32},{296,40},{304,48},{312,... | collective-permute-start | bytes 786440 | tf_op jit(solution)/shard_map/ppermute | solution.py:12
  28.0 0.2 multiply_reduce_fusion.2
  28.4 0.3 fusion.98
  28.7 0.2 fusion.8
  28.8 1.2 %fusion.3 = f32[2,128]{1,0:T(2,128)S(1)} fusion(bf16[2,512,128]{2,1,0:T(8,128)(2,1)} %param.24, f32[2,512,2]{1,2,0:T(2,128)S(1)} %get-tuple-element.16, f32[2,2]{1,0:T(2,128)S(1)} %get-tuple-element.15, pred[2,128]{1,0:T(4,128)(4,1)S(1)} %iota_compare_fusion.3), kind=kOutput, calls=%fused_computation.7 | convolution fusion | flops 529152 | bytes 271632 | tf_op jit(solution)/shard_map/qsh,qsd->qhd/dot_general | solution.py:50
  30.2 0.2 fusion.52
  30.3 0.7 broadcast_in_dim.132
  31.0 5.1 %all-to-all-start.1 = ((f32[8,2,1024]{2,1,0:T(2,128)}), f32[8,2,1024]{2,1,0:T(2,128)S(1)}, u32[]{:S(2)}, u32[]{:S(2)}) async-start(f32[8,2,1024]{2,1,0:T(2,128)} %broadcast_in_dim.132), calls=%async_computation.1 | async-start | bytes 131072 | tf_op jit(solution)/shard_map/all_to_all | solution.py:18
  36.1 4.8 %all-to-all-done.1 = f32[8,2,1024]{2,1,0:T(2,128)S(1)} async-done(((f32[8,2,1024]{2,1,0:T(2,128)}), f32[8,2,1024]{2,1,0:T(2,128)S(1)}, u32[]{:S(2)}, u32[]{:S(2)}) %all-to-all-start.1) | async-done | bytes 65568 | tf_op jit(solution)/shard_map/all_to_all | solution.py:18
  41.1 0.2 multiply_reduce_fusion.1
  41.3 0.3 copy-done.13
  41.7 0.5 fusion.19
  42.2 0.7 broadcast_in_dim.133
  42.9 4.0 %all-to-all-start.2 = ((f32[8,2,1024]{2,1,0:T(2,128)}), f32[8,2,1024]{2,1,0:T(2,128)S(1)}, u32[]{:S(2)}, u32[]{:S(2)}) async-start(f32[8,2,1024]{2,1,0:T(2,128)} %broadcast_in_dim.133), calls=%async_computation.2 | async-start | bytes 131072 | tf_op jit(solution)/shard_map/all_to_all | solution.py:18
  46.9 4.9 %all-to-all-done.2 = f32[8,2,1024]{2,1,0:T(2,128)S(1)} async-done(((f32[8,2,1024]{2,1,0:T(2,128)}), f32[8,2,1024]{2,1,0:T(2,128)S(1)}, u32[]{:S(2)}, u32[]{:S(2)}) %all-to-all-start.2) | async-done | bytes 65568 | tf_op jit(solution)/shard_map/all_to_all | solution.py:18
  51.9 0.2 multiply_reduce_fusion
  52.1 0.3 copy-done.14
  52.5 2.8 %collective-permute-start = (bf16[1,1280]{1,0:T(2,128)(2,1)S(1)}, bf16[1,1280]{1,0:T(2,128)(2,1)S(1)}, u32[]{:S(2)}, u32[]{:S(2)}) collective-permute-start(bf16[1,1280]{1,0:T(2,128)(2,1)S(1)} %pad_maximum_fusion.1), channel_id=1, source_target_pairs={{256,0},{264,8},{272,16},{280,24},{288,32},{296,40},{304,48},{312,... | collective-permute-start | bytes 7688 | tf_op jit(solution)/shard_map/ppermute | solution.py:12
  55.3 10.3 %collective-permute-done = bf16[1,1280]{1,0:T(2,128)(2,1)S(1)} collective-permute-done((bf16[1,1280]{1,0:T(2,128)(2,1)S(1)}, bf16[1,1280]{1,0:T(2,128)(2,1)S(1)}, u32[]{:S(2)}, u32[]{:S(2)}) %collective-permute-start) | collective-permute-done | bytes 2592 | tf_op jit(solution)/shard_map/ppermute | solution.py:12
  65.8 0.5 copy-done.15
  66.3 0.7 %fusion.95 = (bf16[1,512,128]{2,1,0:T(8,128)(2,1)}, bf16[1,512,128]{2,1,0:T(8,128)(2,1)}) fusion(bf16[2,512,128]{2,1,0:T(8,128)(2,1)S(1)} %collective-permute-done.1), kind=kLoop, calls=%fused_computation.145 | loop fusion | bytes 524288 | tf_op jit(solution)/shard_map/slice | solution.py:153
  (78 shorter events, 2.2 us)
Async XLA Ops:
  0.6 41.1 %copy-start = (bf16[512,1024]{1,0:T(8,128)(2,1)S(1)}, bf16[512,1024]{1,0:T(8,128)(2,1)}, u32[]{:S(2)}) copy-start(bf16[512,1024]{1,0:T(8,128)(2,1)} %param.34) | copy-start | bytes 3145732
  0.6 0.8 %copy-start.9 = (bf16[2,1024]{1,0:T(2,128)(2,1)S(1)}, bf16[2,1024]{1,0:T(2,128)(2,1)}, u32[]{:S(2)}) copy-start(bf16[2,1024]{1,0:T(2,128)(2,1)} %param.19) | copy-start | bytes 12292
  0.7 1.9 %copy-start.3 = (bf16[1024,128]{1,0:T(8,128)(2,1)S(1)}, bf16[1024,128]{1,0:T(8,128)(2,1)}, u32[]{:S(2)}) copy-start(bf16[1024,128]{1,0:T(8,128)(2,1)} %param.27) | copy-start | bytes 786436
  1.4 1.3 %copy-start.4 = (bf16[1024,128]{1,0:T(8,128)(2,1)S(1)}, bf16[1024,128]{1,0:T(8,128)(2,1)}, u32[]{:S(2)}) copy-start(bf16[1024,128]{1,0:T(8,128)(2,1)} %param.28) | copy-start | bytes 786436
  2.6 0.7 copy-start.17
  2.6 1.0 %copy-start.2 = (bf16[2,512,128]{2,1,0:T(8,128)(2,1)S(1)}, bf16[2,512,128]{2,1,0:T(8,128)(2,1)}, u32[]{:S(2)}) copy-start(bf16[2,512,128]{2,1,0:T(8,128)(2,1)} %param.20) | copy-start | bytes 786436
  2.7 1.6 %copy-start.10 = (bf16[2,512,128]{2,1,0:T(8,128)(2,1)S(1)}, bf16[2,512,128]{2,1,0:T(8,128)(2,1)}, u32[]{:S(2)}) copy-start(bf16[2,512,128]{2,1,0:T(8,128)(2,1)} %param.21) | copy-start | bytes 786436
  3.5 1.0 %copy-start.5 = (bf16[128,1024]{1,0:T(8,128)(2,1)S(1)}, bf16[128,1024]{1,0:T(8,128)(2,1)}, u32[]{:S(2)}) copy-start(bf16[128,1024]{1,0:T(8,128)(2,1)} %param.30) | copy-start | bytes 786436
  5.4 22.4 %all-to-all-start = ((f32[8,2,1024]{2,1,0:T(2,128)}), f32[8,2,1024]{2,1,0:T(2,128)S(1)}, u32[]{:S(2)}, u32[]{:S(2)}) async-start(f32[8,2,1024]{2,1,0:T(2,128)} %broadcast_in_dim.128), calls=%async_computation | async-start | bytes 131072 | tf_op jit(solution)/shard_map/all_to_all | solution.py:18
  16.1 11.6 %copy-start.18 = (s32[2]{0:T(128)S(1)}, s32[2]{0:T(128)}, u32[]{:S(2)}) copy-start(s32[2]{0:T(128)} %param.25) | copy-start | bytes 28
  16.1 12.0 %copy-start.12 = (f32[1024]{0:T(1024)S(1)}, f32[1024]{0:T(1024)}, u32[]{:S(2)}) copy-start(f32[1024]{0:T(1024)} %param.35) | copy-start | bytes 12292
  16.2 12.1 %copy-start.6 = (bf16[1024,128]{1,0:T(8,128)(2,1)S(1)}, bf16[1024,128]{1,0:T(8,128)(2,1)}, u32[]{:S(2)}) copy-start(bf16[1024,128]{1,0:T(8,128)(2,1)} %param.31) | copy-start | bytes 786436
  16.2 12.2 %copy-start.7 = (bf16[2,512,128]{2,1,0:T(8,128)(2,1)S(1)}, bf16[2,512,128]{2,1,0:T(8,128)(2,1)}, u32[]{:S(2)}) copy-start(bf16[2,512,128]{2,1,0:T(8,128)(2,1)} %param.23) | copy-start | bytes 786436
  16.2 14.0 %copy-start.8 = (bf16[128,1024]{1,0:T(8,128)(2,1)S(1)}, bf16[128,1024]{1,0:T(8,128)(2,1)}, u32[]{:S(2)}) copy-start(bf16[128,1024]{1,0:T(8,128)(2,1)} %param.32) | copy-start | bytes 786436
  16.2 25.5 %copy-start.1 = (bf16[1024,512]{1,0:T(8,128)(2,1)S(1)}, bf16[1024,512]{1,0:T(8,128)(2,1)}, u32[]{:S(2)}) copy-start(bf16[1024,512]{1,0:T(8,128)(2,1)} %param.33) | copy-start | bytes 3145732
  16.3 50.1 %collective-permute-start.1 = (bf16[2,512,128]{2,1,0:T(8,128)(2,1)S(1)}, bf16[2,512,128]{2,1,0:T(8,128)(2,1)S(1)}, u32[]{:S(2)}, u32[]{:S(2)}) collective-permute-start(bf16[2,512,128]{2,1,0:T(8,128)(2,1)S(1)} %pad_maximum_fusion), channel_id=1, source_target_pairs={{256,0},{264,8},{272,16},{280,24},{288,32},{296,40},{304,48},{312,... | collective-permute-start | bytes 786440 | tf_op jit(solution)/shard_map/ppermute | solution.py:12
  31.0 9.9 %all-to-all-start.1 = ((f32[8,2,1024]{2,1,0:T(2,128)}), f32[8,2,1024]{2,1,0:T(2,128)S(1)}, u32[]{:S(2)}, u32[]{:S(2)}) async-start(f32[8,2,1024]{2,1,0:T(2,128)} %broadcast_in_dim.132), calls=%async_computation.1 | async-start | bytes 131072 | tf_op jit(solution)/shard_map/all_to_all | solution.py:18
  40.9 0.7 %copy-start.13 = (f32[1024]{0:T(1024)S(1)}, f32[1024]{0:T(1024)}, u32[]{:S(2)}) copy-start(f32[1024]{0:T(1024)} %param.36) | copy-start | bytes 12292
  42.9 8.9 %all-to-all-start.2 = ((f32[8,2,1024]{2,1,0:T(2,128)}), f32[8,2,1024]{2,1,0:T(2,128)S(1)}, u32[]{:S(2)}, u32[]{:S(2)}) async-start(f32[8,2,1024]{2,1,0:T(2,128)} %broadcast_in_dim.133), calls=%async_computation.2 | async-start | bytes 131072 | tf_op jit(solution)/shard_map/all_to_all | solution.py:18
  51.8 0.7 %copy-start.14 = (f32[1024]{0:T(1024)S(1)}, f32[1024]{0:T(1024)}, u32[]{:S(2)}) copy-start(f32[1024]{0:T(1024)} %param.37) | copy-start | bytes 12292
  52.5 13.1 %collective-permute-start = (bf16[1,1280]{1,0:T(2,128)(2,1)S(1)}, bf16[1,1280]{1,0:T(2,128)(2,1)S(1)}, u32[]{:S(2)}, u32[]{:S(2)}) collective-permute-start(bf16[1,1280]{1,0:T(2,128)(2,1)S(1)} %pad_maximum_fusion.1), channel_id=1, source_target_pairs={{256,0},{264,8},{272,16},{280,24},{288,32},{296,40},{304,48},{312,... | collective-permute-start | bytes 7688 | tf_op jit(solution)/shard_map/ppermute | solution.py:12
  65.7 0.6 copy-start.11
  65.8 0.5 copy-start.15
  66.3 0.7 %copy-start.16 = (bf16[2,128]{1,0:T(2,128)(2,1)}, bf16[2,128]{1,0:T(2,128)(2,1)S(1)}, u32[]{:S(2)}) copy-start(bf16[2,128]{1,0:T(2,128)(2,1)S(1)} %dynamic_update_slice.10) | copy-start | bytes 1540

commit v7 on v4

--- a/solution.py
+++ b/solution.py
@@ -105,10 +105,6 @@
 
 def take_slot(array, chosen):
     return lax.dynamic_slice_in_dim(array, chosen, 1, 0)
-
-
-def put_slot(array, row, chosen):
-    return lax.dynamic_update_slice_in_dim(array, row, chosen, 0)
 
 
 def on_device(
@@ -147,34 +143,27 @@
     )
     chosen = give_slot[0]
     half_axis = lax.axis_size("req") // 2
+    count, span, part = self_keys.shape
     layer_out, fresh_keys, fresh_values = decode_layer(
         tokens, self_keys, self_values, self_len, cross_keys, cross_values, cross_len, params
     )
-    count, span, part = self_keys.shape
-    width = layer_out.shape[1]
-    rows = jnp.concatenate(
-        (
-            take_slot(layer_out, chosen),
-            take_slot(fresh_keys, chosen),
-            take_slot(fresh_values, chosen),
-        ),
-        axis=1,
-    ).reshape(-1, part)
     parcel = jnp.concatenate(
         (
             take_slot(self_keys, chosen).reshape(span, part),
             take_slot(self_values, chosen).reshape(span, part),
-            rows,
+            take_slot(fresh_keys, chosen),
+            take_slot(fresh_values, chosen),
         ),
         axis=0,
     )
     arrived = passed_along(parcel, "req", half_axis)
     moved_keys = arrived[:span].reshape(1, span, part)
     moved_values = arrived[span : 2 * span].reshape(1, span, part)
-    arrived_rows = arrived[2 * span :].reshape(1, -1)
-    decoded = put_slot(layer_out, arrived_rows[:, :width], chosen)
-    new_keys = put_slot(fresh_keys, arrived_rows[:, width : width + part], chosen)
-    new_values = put_slot(fresh_values, arrived_rows[:, width + part :], chosen)
+    here = (lax.iota(jnp.int32, count) == chosen)[:, None]
+    new_keys = jnp.where(here, arrived[2 * span : 2 * span + 1], fresh_keys)
+    new_values = jnp.where(here, arrived[2 * span + 1 :], fresh_values)
+    row = passed_along(take_slot(layer_out, chosen), "req", half_axis)
+    decoded = jnp.where(here, row, layer_out)
     return (decoded, new_keys, new_values, moved_keys, moved_values)
 
 
@@ -200,7 +189,7 @@
         P(),
         P(),
     )
-    step = jax.shard_map(
+    return jax.shard_map(
         on_device,
         mesh=mesh,
         in_specs=placed,
@@ -213,4 +202,3 @@
         ),
         check_vma=False,
     )
-    return step

time: 81.8 us -> 76.9 us (0.940)
  the two profiles are of different devices: /device:TPU:38 before, /device:TPU:46 now
where the time goes in v7:
time: 76.9 us; the launch traced here: 76.3 us
  starting transfers between devices  33.4 us (43%)
  waiting for transfers between devices  25 us (33%)
  local copies, waits for them, and re-layouts  8.2 us (11%)
  matrix products  4.73 us (6%)
  other arithmetic  3.47 us (5%)
  between operations  1.46 us (2%)
    ppermute x2, waiting for transfers between devices, passed_along(): return lax.ppermute(block, axis, route)  19.2 us
    ppermute x2, starting transfers between devices, passed_along(): return lax.ppermute(block, axis, route)  18.9 us
    all_to_all x3, starting transfers between devices, head_sum(): gathered = lax.all_to_all(spread, 'head', 0, 0)  14.5 us
    all_to_all x3, waiting for transfers between devices, head_sum(): gathered = lax.all_to_all(spread, 'head', 0, 0)  5.81 us
    unnamed x38, local copies, waits for them, and re-layouts  4.79 us
    broadcast_in_dim x3, local copies, waits for them, and re-layouts, head_sum(): spread = jnp.broadcast_to(value[None], (count,) + value.shape)  1.96 us
  transfers between devices with their start and end apart: 5, of which 3 were waited for; matrix products, arithmetic and copies ran while one was open for 3% of the time, Pallas kernels for 0%

profile of v7, /device:TPU:46, one launch (start us, length us, event | category | flops | bytes accessed | tf_op | source)
XLA Modules:
  0.0 76.3 jit_solution(15172479951811207364)
XLA Ops:
  0.7 1.2 %fusion.3 = bf16[2,128]{1,0:T(2,128)(2,1)S(1)} fusion(bf16[2,1024]{1,0:T(2,128)(2,1)} %param.19, bf16[1024,128]{1,0:T(8,128)(2,1)} %param.27), kind=kOutput, calls=%fused_computation.5 | convolution fusion | flops 524800 | bytes 266752 | tf_op jit(solution)/shard_map/dot_general | solution.py:82
  2.1 0.8 %convolution_convert_fusion.1 = bf16[2,128]{1,0:T(2,128)(2,1)S(1)} fusion(bf16[2,1024]{1,0:T(2,128)(2,1)} %param.19, bf16[1024,128]{1,0:T(8,128)(2,1)S(1)} %copy-done.4), kind=kOutput, calls=%fused_computation.8 | convolution fusion | flops 524544 | bytes 266752 | tf_op jit(solution)/shard_map/dot_general | solution.py:85
  3.2 0.5 copy-done.15
  4.1 0.2 fusion.9
  4.3 0.4 copy-done.2
  4.8 0.8 %copy-done.5 = bf16[1024,128]{1,0:T(8,128)(2,1)S(1)} copy-done((bf16[1024,128]{1,0:T(8,128)(2,1)S(1)}, bf16[1024,128]{1,0:T(8,128)(2,1)}, u32[]{:S(2)}) %copy-start.5) | copy-done | bytes 262168
  5.8 0.2 fusion.7
  6.1 0.4 copy-done.6
  6.7 0.7 broadcast_in_dim.104
  7.3 5.0 %all-to-all-start = ((f32[8,2,1024]{2,1,0:T(2,128)}), f32[8,2,1024]{2,1,0:T(2,128)S(1)}, u32[]{:S(2)}, u32[]{:S(2)}) async-start(f32[8,2,1024]{2,1,0:T(2,128)} %broadcast_in_dim.104), calls=%async_computation | async-start | bytes 131072 | tf_op jit(solution)/shard_map/all_to_all | solution.py:18
  12.6 0.8 %copy-done.8 = bf16[2,512,128]{2,1,0:T(8,128)(2,1)S(1)} copy-done((bf16[2,512,128]{2,1,0:T(8,128)(2,1)S(1)}, bf16[2,512,128]{2,1,0:T(8,128)(2,1)}, u32[]{:S(2)}) %copy-start.8) | copy-done | bytes 262168
  13.4 0.8 %copy.36 = bf16[2,512,128]{1,2,0:T(8,128)(2,1)} copy(bf16[2,512,128]{2,1,0:T(8,128)(2,1)S(1)} %copy-done.8) | data formatting | bytes 524288 | tf_op args[5]
  14.9 1.6 %all-to-all-done = f32[8,2,1024]{2,1,0:T(2,128)S(1)} async-done(((f32[8,2,1024]{2,1,0:T(2,128)}), f32[8,2,1024]{2,1,0:T(2,128)S(1)}, u32[]{:S(2)}, u32[]{:S(2)}) %all-to-all-start) | async-done | bytes 65568 | tf_op jit(solution)/shard_map/all_to_all | solution.py:18
  16.7 0.2 multiply_reduce_fusion.2
  17.6 1.1 %fusion.5 = f32[2,2,1,64]{3,2,1,0:T(1,128)S(1)} fusion(bf16[2,512,2,64]{1,3,2,0:T(8,128)(2,1)} %bitcast.65, bf16[2,2,512,1]{2,1,0,3:T(2,128)(2,1)S(1)} %get-tuple-element.14), kind=kOutput, calls=%fused_computation.15 | convolution fusion | flops 262144 | bytes 267264 | tf_op jit(solution)/shard_map/qhs,qshd->qhd/dot_general | solution.py:50
  18.9 0.2 fusion.93
  19.0 0.7 broadcast_in_dim.106
  19.7 4.7 %all-to-all-start.1 = ((f32[8,2,1024]{2,1,0:T(2,128)}), f32[8,2,1024]{2,1,0:T(2,128)S(1)}, u32[]{:S(2)}, u32[]{:S(2)}) async-start(f32[8,2,1024]{2,1,0:T(2,128)} %broadcast_in_dim.106), calls=%async_computation.1 | async-start | bytes 131072 | tf_op jit(solution)/shard_map/all_to_all | solution.py:18
  24.4 4.2 %all-to-all-done.1 = f32[8,2,1024]{2,1,0:T(2,128)S(1)} async-done(((f32[8,2,1024]{2,1,0:T(2,128)}), f32[8,2,1024]{2,1,0:T(2,128)S(1)}, u32[]{:S(2)}, u32[]{:S(2)}) %all-to-all-start.1) | async-done | bytes 65568 | tf_op jit(solution)/shard_map/all_to_all | solution.py:18
  28.8 0.2 multiply_reduce_fusion.1
  29.0 0.3 copy-done.13
  29.4 0.5 fusion.18
  29.9 0.7 broadcast_in_dim.107
  30.5 4.7 %all-to-all-start.2 = ((f32[8,2,1024]{2,1,0:T(2,128)}), f32[8,2,1024]{2,1,0:T(2,128)S(1)}, u32[]{:S(2)}, u32[]{:S(2)}) async-start(f32[8,2,1024]{2,1,0:T(2,128)} %broadcast_in_dim.107), calls=%async_computation.2 | async-start | bytes 131072 | tf_op jit(solution)/shard_map/all_to_all | solution.py:18
  35.3 14.8 %collective-permute-start.1 = (bf16[1026,128]{1,0:T(8,128)(2,1)S(1)}, bf16[1026,128]{1,0:T(8,128)(2,1)S(1)}, u32[]{:S(2)}, u32[]{:S(2)}) collective-permute-start(bf16[1026,128]{1,0:T(8,128)(2,1)S(1)} %concatenate.3), channel_id=1, source_target_pairs={{256,0},{264,8},{272,16},{280,24},{288,32},{296,40},{304,48},{312,... | collective-permute-start | bytes 787976 | tf_op jit(solution)/shard_map/ppermute | solution.py:12
  50.3 0.2 multiply_reduce_fusion
  50.5 0.3 copy-done.14
  50.9 4.1 %collective-permute-start = (bf16[1,1024]{1,0:T(2,128)(2,1)S(1)}, bf16[1,1024]{1,0:T(2,128)(2,1)S(1)}, u32[]{:S(2)}, u32[]{:S(2)}) collective-permute-start(bf16[1,1024]{1,0:T(2,128)(2,1)S(1)} %constant_dynamic-slice_fusion.2), channel_id=1, source_target_pairs={{256,0},{264,8},{272,16},{280,24},{288,32},{296,40},{304,48},{312,... | collective-permute-start | bytes 6152 | tf_op jit(solution)/shard_map/ppermute | solution.py:12
  55.1 19.2 %collective-permute-done = bf16[1,1024]{1,0:T(2,128)(2,1)S(1)} collective-permute-done((bf16[1,1024]{1,0:T(2,128)(2,1)S(1)}, bf16[1,1024]{1,0:T(2,128)(2,1)S(1)}, u32[]{:S(2)}, u32[]{:S(2)}) %collective-permute-start) | collective-permute-done | bytes 2080 | tf_op jit(solution)/shard_map/ppermute | solution.py:12
  74.3 0.7 broadcast_select_fusion
  75.0 0.6 broadcast_select_fusion.1
  75.6 0.7 slice_bitcast_fusion
  (76 shorter events, 3.4 us)
Async XLA Ops:
  0.6 28.7 %copy-start = (bf16[512,1024]{1,0:T(8,128)(2,1)S(1)}, bf16[512,1024]{1,0:T(8,128)(2,1)}, u32[]{:S(2)}) copy-start(bf16[512,1024]{1,0:T(8,128)(2,1)} %param.34) | copy-start | bytes 3145732
  0.6 1.4 %copy-start.4 = (bf16[1024,128]{1,0:T(8,128)(2,1)S(1)}, bf16[1024,128]{1,0:T(8,128)(2,1)}, u32[]{:S(2)}) copy-start(bf16[1024,128]{1,0:T(8,128)(2,1)} %param.28) | copy-start | bytes 786436
  0.7 2.3 %copy-start.3 = (bf16[2,512,128]{2,1,0:T(8,128)(2,1)S(1)}, bf16[2,512,128]{2,1,0:T(8,128)(2,1)}, u32[]{:S(2)}) copy-start(bf16[2,512,128]{2,1,0:T(8,128)(2,1)} %param.20) | copy-start | bytes 786436
  3.0 0.7 copy-start.15
  3.7 0.9 %copy-start.2 = (bf16[2,512,128]{2,1,0:T(8,128)(2,1)S(1)}, bf16[2,512,128]{2,1,0:T(8,128)(2,1)}, u32[]{:S(2)}) copy-start(bf16[2,512,128]{2,1,0:T(8,128)(2,1)} %param.21) | copy-start | bytes 786436
  4.6 0.9 %copy-start.5 = (bf16[1024,128]{1,0:T(8,128)(2,1)S(1)}, bf16[1024,128]{1,0:T(8,128)(2,1)}, u32[]{:S(2)}) copy-start(bf16[1024,128]{1,0:T(8,128)(2,1)} %param.29) | copy-start | bytes 786436
  4.6 1.0 %copy-start.11 = (bf16[2,1024]{1,0:T(2,128)(2,1)S(1)}, bf16[2,1024]{1,0:T(2,128)(2,1)}, u32[]{:S(2)}) copy-start(bf16[2,1024]{1,0:T(2,128)(2,1)} %param.19) | copy-start | bytes 12292
  5.6 1.0 %copy-start.6 = (bf16[128,1024]{1,0:T(8,128)(2,1)S(1)}, bf16[128,1024]{1,0:T(8,128)(2,1)}, u32[]{:S(2)}) copy-start(bf16[128,1024]{1,0:T(8,128)(2,1)} %param.30) | copy-start | bytes 786436
  6.0 6.5 %copy-start.7 = (bf16[2,512,128]{2,1,0:T(8,128)(2,1)S(1)}, bf16[2,512,128]{2,1,0:T(8,128)(2,1)}, u32[]{:S(2)}) copy-start(bf16[2,512,128]{2,1,0:T(8,128)(2,1)} %param.23) | copy-start | bytes 786436
  7.3 5.1 %copy-start.16 = (s32[2]{0:T(128)S(1)}, s32[2]{0:T(128)}, u32[]{:S(2)}) copy-start(s32[2]{0:T(128)} %param.25) | copy-start | bytes 28
  7.3 9.2 %all-to-all-start = ((f32[8,2,1024]{2,1,0:T(2,128)}), f32[8,2,1024]{2,1,0:T(2,128)S(1)}, u32[]{:S(2)}, u32[]{:S(2)}) async-start(f32[8,2,1024]{2,1,0:T(2,128)} %broadcast_in_dim.104), calls=%async_computation | async-start | bytes 131072 | tf_op jit(solution)/shard_map/all_to_all | solution.py:18
  12.4 1.0 %copy-start.8 = (bf16[2,512,128]{2,1,0:T(8,128)(2,1)S(1)}, bf16[2,512,128]{2,1,0:T(8,128)(2,1)}, u32[]{:S(2)}) copy-start(bf16[2,512,128]{2,1,0:T(8,128)(2,1)} %param.24) | copy-start | bytes 786436
  13.4 3.5 %copy-start.12 = (f32[1024]{0:T(1024)S(1)}, f32[1024]{0:T(1024)}, u32[]{:S(2)}) copy-start(f32[1024]{0:T(1024)} %param.35) | copy-start | bytes 12292
  13.4 3.6 %copy-start.9 = (bf16[1024,128]{1,0:T(8,128)(2,1)S(1)}, bf16[1024,128]{1,0:T(8,128)(2,1)}, u32[]{:S(2)}) copy-start(bf16[1024,128]{1,0:T(8,128)(2,1)} %param.31) | copy-start | bytes 786436
  16.5 2.3 %copy-start.10 = (bf16[128,1024]{1,0:T(8,128)(2,1)S(1)}, bf16[128,1024]{1,0:T(8,128)(2,1)}, u32[]{:S(2)}) copy-start(bf16[128,1024]{1,0:T(8,128)(2,1)} %param.32) | copy-start | bytes 786436
  16.6 12.8 %copy-start.1 = (bf16[1024,512]{1,0:T(8,128)(2,1)S(1)}, bf16[1024,512]{1,0:T(8,128)(2,1)}, u32[]{:S(2)}) copy-start(bf16[1024,512]{1,0:T(8,128)(2,1)} %param.33) | copy-start | bytes 3145732
  19.7 8.9 %all-to-all-start.1 = ((f32[8,2,1024]{2,1,0:T(2,128)}), f32[8,2,1024]{2,1,0:T(2,128)S(1)}, u32[]{:S(2)}, u32[]{:S(2)}) async-start(f32[8,2,1024]{2,1,0:T(2,128)} %broadcast_in_dim.106), calls=%async_computation.1 | async-start | bytes 131072 | tf_op jit(solution)/shard_map/all_to_all | solution.py:18
  28.6 0.7 copy-start.13
  30.5 19.6 %all-to-all-start.2 = ((f32[8,2,1024]{2,1,0:T(2,128)}), f32[8,2,1024]{2,1,0:T(2,128)S(1)}, u32[]{:S(2)}, u32[]{:S(2)}) async-start(f32[8,2,1024]{2,1,0:T(2,128)} %broadcast_in_dim.107), calls=%async_computation.2 | async-start | bytes 131072 | tf_op jit(solution)/shard_map/all_to_all | solution.py:18
  35.3 39.6 %collective-permute-start.1 = (bf16[1026,128]{1,0:T(8,128)(2,1)S(1)}, bf16[1026,128]{1,0:T(8,128)(2,1)S(1)}, u32[]{:S(2)}, u32[]{:S(2)}) collective-permute-start(bf16[1026,128]{1,0:T(8,128)(2,1)S(1)} %concatenate.3), channel_id=1, source_target_pairs={{256,0},{264,8},{272,16},{280,24},{288,32},{296,40},{304,48},{312,... | collective-permute-start | bytes 787976 | tf_op jit(solution)/shard_map/ppermute | solution.py:12
  50.2 0.7 copy-start.14
  50.9 23.3 %collective-permute-start = (bf16[1,1024]{1,0:T(2,128)(2,1)S(1)}, bf16[1,1024]{1,0:T(2,128)(2,1)S(1)}, u32[]{:S(2)}, u32[]{:S(2)}) collective-permute-start(bf16[1,1024]{1,0:T(2,128)(2,1)S(1)} %constant_dynamic-slice_fusion.2), channel_id=1, source_target_pairs={{256,0},{264,8},{272,16},{280,24},{288,32},{296,40},{304,48},{312,... | collective-permute-start | bytes 6152 | tf_op jit(solution)/shard_map/ppermute | solution.py:12

commit v8 on v7

--- a/solution.py
+++ b/solution.py
@@ -12,11 +12,13 @@
     return lax.ppermute(block, axis, route)
 
 
-def head_sum(value):
+def head_sum(value, tie=None):
     count = lax.axis_size("head")
     spread = jnp.broadcast_to(value[None], (count,) + value.shape)
+    if tie is not None:
+        tie, spread = lax.optimization_barrier((tie, spread))
     gathered = lax.all_to_all(spread, "head", 0, 0)
-    return jnp.sum(gathered, axis=0)
+    return jnp.sum(gathered, axis=0), tie
 
 
 def layer_norm(value, gain):
@@ -63,7 +65,7 @@
 
 
 def decode_layer(
-    tokens, self_keys, self_values, self_len, cross_keys, cross_values, cross_len, params
+    tokens, self_keys, self_values, self_len, cross_keys, cross_values, cross_len, params, tie=None
 ):
     (
         w_query,
@@ -85,22 +87,22 @@
     fresh_keys = jnp.dot(tokens, w_key, preferred_element_type=jnp.float32).astype(jnp.bfloat16)
     fresh_values = jnp.dot(tokens, w_value, preferred_element_type=jnp.float32).astype(jnp.bfloat16)
     self_mixed = attend(query, self_keys, self_values, self_len, fresh_keys, fresh_values)
-    self_total = head_sum(jnp.dot(self_mixed, w_out, preferred_element_type=jnp.float32))
+    self_total, tie = head_sum(jnp.dot(self_mixed, w_out, preferred_element_type=jnp.float32), tie)
     first = layer_norm(tokens.astype(jnp.float32) + self_total, gain_self).astype(jnp.bfloat16)
     cross_query = (
         jnp.dot(first, w_cross_query, preferred_element_type=jnp.float32) * scale
     ).astype(jnp.bfloat16)
     cross_mixed = attend(cross_query, cross_keys, cross_values, cross_len, None, None)
-    cross_total = head_sum(
+    cross_total, _ = head_sum(
         jnp.dot(cross_mixed, w_cross_out, preferred_element_type=jnp.float32)
     )
     second = layer_norm(first.astype(jnp.float32) + cross_total, gain_cross).astype(jnp.bfloat16)
     hidden = jax.nn.gelu(
         jnp.dot(second, w_up, preferred_element_type=jnp.float32), approximate=False
     ).astype(jnp.bfloat16)
-    ffn_total = head_sum(jnp.dot(hidden, w_down, preferred_element_type=jnp.float32))
+    ffn_total, _ = head_sum(jnp.dot(hidden, w_down, preferred_element_type=jnp.float32))
     layer_out = layer_norm(second.astype(jnp.float32) + ffn_total, gain_final).astype(jnp.bfloat16)
-    return (layer_out, fresh_keys, fresh_values)
+    return (layer_out, fresh_keys, fresh_values, tie)
 
 
 def take_slot(array, chosen):
@@ -143,14 +145,15 @@
     )
     chosen = give_slot[0]
     half_axis = lax.axis_size("req") // 2
+    caches = jnp.concatenate((take_slot(self_keys, chosen), take_slot(self_values, chosen)), axis=0)
+    layer_out, fresh_keys, fresh_values, caches = decode_layer(
+        tokens, self_keys, self_values, self_len, cross_keys, cross_values, cross_len, params,
+        caches,
+    )
     count, span, part = self_keys.shape
-    layer_out, fresh_keys, fresh_values = decode_layer(
-        tokens, self_keys, self_values, self_len, cross_keys, cross_values, cross_len, params
-    )
     parcel = jnp.concatenate(
         (
-            take_slot(self_keys, chosen).reshape(span, part),
-            take_slot(self_values, chosen).reshape(span, part),
+            caches.reshape(2 * span, part),
             take_slot(fresh_keys, chosen),
             take_slot(fresh_values, chosen),
         ),

time: 76.9 us -> 76 us (0.988)
  blocking collectives: 0 us -> 8 us
  starting transfers between devices: 33.4 us -> 28.6 us
  waiting for transfers between devices: 25 us -> 22.2 us
  matrix products: 4.73 us -> 3.77 us
    all_to_all x0 -> x1, blocking collectives: none -> 8 us  [head_sum(): gathered = lax.all_to_all(spread, 'head', 0, 0)]
    all_to_all x3 -> x2, starting transfers between devices: 14.5 us -> 9.76 us  [head_sum(): gathered = lax.all_to_all(spread, 'head', 0, 0)]
    all_to_all x3 -> x2, waiting for transfers between devices: 5.81 us -> 2.99 us  [head_sum(): gathered = lax.all_to_all(spread, 'head', 0, 0)]
    dot_general x2, matrix products: 1.28 us -> 0.33 us  [attend(): jnp.einsum('qhs,qshd->qhd', weights.astype(jnp.bfloat16), value_heads, pr...]
  transfers between devices with their start and end apart: 5 -> 4, of which waited for: 3 -> 2; matrix products, arithmetic and copies ran while one was open for 3% -> 2% of each run, Pallas kernels for 0% -> 0%
where the time goes in v8:
time: 76 us; the launch traced here: 75.4 us
  starting transfers between devices  28.6 us (38%)
  waiting for transfers between devices  22.2 us (29%)
  blocking collectives  8 us (11%)
  local copies, waits for them, and re-layouts  7.73 us (10%)
  matrix products  3.77 us (5%)
  other arithmetic  3.5 us (5%)
  between operations  1.51 us (2%)
    ppermute x2, waiting for transfers between devices, passed_along(): return lax.ppermute(block, axis, route)  19.3 us
    ppermute x2, starting transfers between devices, passed_along(): return lax.ppermute(block, axis, route)  18.8 us
    all_to_all x2, starting transfers between devices, head_sum(): gathered = lax.all_to_all(spread, 'head', 0, 0)  9.76 us
    all_to_all x1, blocking collectives, head_sum(): gathered = lax.all_to_all(spread, 'head', 0, 0)  8 us
    unnamed x38, local copies, waits for them, and re-layouts  4.9 us
    all_to_all x2, waiting for transfers between devices, head_sum(): gathered = lax.all_to_all(spread, 'head', 0, 0)  2.99 us
  transfers between devices with their start and end apart: 4, of which 2 were waited for; matrix products, arithmetic and copies ran while one was open for 2% of the time, Pallas kernels for 0%

profile of v8, /device:TPU:46, one launch (start us, length us, event | category | flops | bytes accessed | tf_op | source)
XLA Modules:
  0.0 75.4 jit_solution(11830214865578214309)
XLA Ops:
  0.7 1.2 %fusion.3 = bf16[2,128]{1,0:T(2,128)(2,1)S(1)} fusion(bf16[2,1024]{1,0:T(2,128)(2,1)} %param.19, bf16[1024,128]{1,0:T(8,128)(2,1)} %param.27), kind=kOutput, calls=%fused_computation.5 | convolution fusion | flops 524800 | bytes 266752 | tf_op jit(solution)/shard_map/dot_general | solution.py:84
  2.1 0.8 %convolution_convert_fusion.1 = bf16[2,128]{1,0:T(2,128)(2,1)S(1)} fusion(bf16[2,1024]{1,0:T(2,128)(2,1)} %param.19, bf16[1024,128]{1,0:T(8,128)(2,1)S(1)} %copy-done.4), kind=kOutput, calls=%fused_computation.8 | convolution fusion | flops 524544 | bytes 266752 | tf_op jit(solution)/shard_map/dot_general | solution.py:87
  3.0 0.2 copy.32
  3.2 0.5 copy-done.15
  4.1 0.2 fusion.9
  4.3 0.4 copy-done.2
  4.8 0.8 %copy-done.5 = bf16[1024,128]{1,0:T(8,128)(2,1)S(1)} copy-done((bf16[1024,128]{1,0:T(8,128)(2,1)S(1)}, bf16[1024,128]{1,0:T(8,128)(2,1)}, u32[]{:S(2)}) %copy-start.5) | copy-done | bytes 262168
  5.8 0.2 fusion.7
  6.9 0.9 %copy-done.6 = bf16[128,1024]{1,0:T(8,128)(2,1)S(1)} copy-done((bf16[128,1024]{1,0:T(8,128)(2,1)S(1)}, bf16[128,1024]{1,0:T(8,128)(2,1)}, u32[]{:S(2)}) %copy-start.6) | copy-done | bytes 262168
  7.9 0.6 broadcast_in_dim.104
  8.6 5.0 %all-to-all-start = ((f32[8,2,1024]{2,1,0:T(2,128)}), f32[8,2,1024]{2,1,0:T(2,128)S(1)}, u32[]{:S(2)}, u32[]{:S(2)}) async-start(f32[8,2,1024]{2,1,0:T(2,128)} %broadcast_in_dim.104), calls=%async_computation | async-start | bytes 131072 | tf_op jit(solution)/shard_map/all_to_all | solution.py:20
  13.9 0.8 %copy-done.8 = bf16[2,512,128]{2,1,0:T(8,128)(2,1)S(1)} copy-done((bf16[2,512,128]{2,1,0:T(8,128)(2,1)S(1)}, bf16[2,512,128]{2,1,0:T(8,128)(2,1)}, u32[]{:S(2)}) %copy-start.8) | copy-done | bytes 262168
  14.8 3.0 %all-to-all-done = f32[8,2,1024]{2,1,0:T(2,128)S(1)} async-done(((f32[8,2,1024]{2,1,0:T(2,128)}), f32[8,2,1024]{2,1,0:T(2,128)S(1)}, u32[]{:S(2)}, u32[]{:S(2)}) %all-to-all-start) | async-done | bytes 65568 | tf_op jit(solution)/shard_map/all_to_all | solution.py:20
  18.0 0.2 multiply_reduce_fusion.2
  18.3 0.1 fusion.4
  18.8 0.2 fusion.5
  19.2 0.3 copy-done.10
  19.5 0.1 fusion.93
  19.6 8.0 %all_to_all.15 = f32[8,2,1024]{2,1,0:T(2,128)S(1)} all-to-all(f32[8,2,1024]{2,1,0:T(2,128)S(1)} %broadcast_in_dim.106), channel_id=1, replica_groups=mesh['req'=64,'head'=8] {'head'}, dimensions={0} | all-to-all | bytes 131072 | tf_op jit(solution)/shard_map/all_to_all | solution.py:20
  27.8 0.2 multiply_reduce_fusion.1
  28.0 0.3 copy-done.13
  28.4 0.5 fusion.18
  28.9 0.7 broadcast_in_dim.107
  29.6 4.7 %all-to-all-start.2 = ((f32[8,2,1024]{2,1,0:T(2,128)}), f32[8,2,1024]{2,1,0:T(2,128)S(1)}, u32[]{:S(2)}, u32[]{:S(2)}) async-start(f32[8,2,1024]{2,1,0:T(2,128)} %broadcast_in_dim.107), calls=%async_computation.2 | async-start | bytes 131072 | tf_op jit(solution)/shard_map/all_to_all | solution.py:20
  34.4 14.8 %collective-permute-start.1 = (bf16[1026,128]{1,0:T(8,128)(2,1)S(1)}, bf16[1026,128]{1,0:T(8,128)(2,1)S(1)}, u32[]{:S(2)}, u32[]{:S(2)}) collective-permute-start(bf16[1026,128]{1,0:T(8,128)(2,1)S(1)} %concatenate.7), channel_id=1, source_target_pairs={{256,0},{264,8},{272,16},{280,24},{288,32},{296,40},{304,48},{312,... | collective-permute-start | bytes 787976 | tf_op jit(solution)/shard_map/ppermute | solution.py:12
  49.4 0.2 multiply_reduce_fusion
  49.6 0.3 copy-done.14
  50.0 4.0 %collective-permute-start = (bf16[1,1024]{1,0:T(2,128)(2,1)S(1)}, bf16[1,1024]{1,0:T(2,128)(2,1)S(1)}, u32[]{:S(2)}, u32[]{:S(2)}) collective-permute-start(bf16[1,1024]{1,0:T(2,128)(2,1)S(1)} %constant_dynamic-slice_fusion.2), channel_id=1, source_target_pairs={{256,0},{264,8},{272,16},{280,24},{288,32},{296,40},{304,48},{312,... | collective-permute-start | bytes 6152 | tf_op jit(solution)/shard_map/ppermute | solution.py:12
  54.1 19.3 %collective-permute-done = bf16[1,1024]{1,0:T(2,128)(2,1)S(1)} collective-permute-done((bf16[1,1024]{1,0:T(2,128)(2,1)S(1)}, bf16[1,1024]{1,0:T(2,128)(2,1)S(1)}, u32[]{:S(2)}, u32[]{:S(2)}) %collective-permute-start) | collective-permute-done | bytes 2080 | tf_op jit(solution)/shard_map/ppermute | solution.py:12
  73.4 0.7 broadcast_select_fusion
  74.1 0.6 broadcast_select_fusion.1
  74.6 0.7 slice_bitcast_fusion
  (76 shorter events, 3.4 us)
Async XLA Ops:
  0.6 27.8 %copy-start = (bf16[512,1024]{1,0:T(8,128)(2,1)S(1)}, bf16[512,1024]{1,0:T(8,128)(2,1)}, u32[]{:S(2)}) copy-start(bf16[512,1024]{1,0:T(8,128)(2,1)} %param.34) | copy-start | bytes 3145732
  0.6 1.4 %copy-start.4 = (bf16[1024,128]{1,0:T(8,128)(2,1)S(1)}, bf16[1024,128]{1,0:T(8,128)(2,1)}, u32[]{:S(2)}) copy-start(bf16[1024,128]{1,0:T(8,128)(2,1)} %param.28) | copy-start | bytes 786436
  0.7 2.3 %copy-start.3 = (bf16[2,512,128]{2,1,0:T(8,128)(2,1)S(1)}, bf16[2,512,128]{2,1,0:T(8,128)(2,1)}, u32[]{:S(2)}) copy-start(bf16[2,512,128]{2,1,0:T(8,128)(2,1)} %param.20) | copy-start | bytes 786436
  3.0 0.7 copy-start.15
  3.7 0.9 %copy-start.2 = (bf16[2,512,128]{2,1,0:T(8,128)(2,1)S(1)}, bf16[2,512,128]{2,1,0:T(8,128)(2,1)}, u32[]{:S(2)}) copy-start(bf16[2,512,128]{2,1,0:T(8,128)(2,1)} %param.21) | copy-start | bytes 786436
  4.6 0.9 %copy-start.5 = (bf16[1024,128]{1,0:T(8,128)(2,1)S(1)}, bf16[1024,128]{1,0:T(8,128)(2,1)}, u32[]{:S(2)}) copy-start(bf16[1024,128]{1,0:T(8,128)(2,1)} %param.29) | copy-start | bytes 786436
  4.6 1.0 %copy-start.11 = (bf16[2,1024]{1,0:T(2,128)(2,1)S(1)}, bf16[2,1024]{1,0:T(2,128)(2,1)}, u32[]{:S(2)}) copy-start(bf16[2,1024]{1,0:T(2,128)(2,1)} %param.19) | copy-start | bytes 12292
  6.8 1.0 %copy-start.6 = (bf16[128,1024]{1,0:T(8,128)(2,1)S(1)}, bf16[128,1024]{1,0:T(8,128)(2,1)}, u32[]{:S(2)}) copy-start(bf16[128,1024]{1,0:T(8,128)(2,1)} %param.30) | copy-start | bytes 786436
  7.9 5.8 %copy-start.7 = (bf16[2,512,128]{2,1,0:T(8,128)(2,1)S(1)}, bf16[2,512,128]{2,1,0:T(8,128)(2,1)}, u32[]{:S(2)}) copy-start(bf16[2,512,128]{2,1,0:T(8,128)(2,1)} %param.23) | copy-start | bytes 786436
  8.6 5.1 %copy-start.16 = (s32[2]{0:T(128)S(1)}, s32[2]{0:T(128)}, u32[]{:S(2)}) copy-start(s32[2]{0:T(128)} %param.25) | copy-start | bytes 28
  8.6 9.2 %all-to-all-start = ((f32[8,2,1024]{2,1,0:T(2,128)}), f32[8,2,1024]{2,1,0:T(2,128)S(1)}, u32[]{:S(2)}, u32[]{:S(2)}) async-start(f32[8,2,1024]{2,1,0:T(2,128)} %broadcast_in_dim.104), calls=%async_computation | async-start | bytes 131072 | tf_op jit(solution)/shard_map/all_to_all | solution.py:20
  13.7 1.0 %copy-start.8 = (bf16[2,512,128]{2,1,0:T(8,128)(2,1)S(1)}, bf16[2,512,128]{2,1,0:T(8,128)(2,1)}, u32[]{:S(2)}) copy-start(bf16[2,512,128]{2,1,0:T(8,128)(2,1)} %param.24) | copy-start | bytes 786436
  13.7 4.5 %copy-start.12 = (f32[1024]{0:T(1024)S(1)}, f32[1024]{0:T(1024)}, u32[]{:S(2)}) copy-start(f32[1024]{0:T(1024)} %param.35) | copy-start | bytes 12292
  13.7 4.5 %copy-start.9 = (bf16[1024,128]{1,0:T(8,128)(2,1)S(1)}, bf16[1024,128]{1,0:T(8,128)(2,1)}, u32[]{:S(2)}) copy-start(bf16[1024,128]{1,0:T(8,128)(2,1)} %param.31) | copy-start | bytes 786436
  14.7 13.7 %copy-start.1 = (bf16[1024,512]{1,0:T(8,128)(2,1)S(1)}, bf16[1024,512]{1,0:T(8,128)(2,1)}, u32[]{:S(2)}) copy-start(bf16[1024,512]{1,0:T(8,128)(2,1)} %param.33) | copy-start | bytes 3145732
  18.5 1.0 %copy-start.10 = (bf16[128,1024]{1,0:T(8,128)(2,1)S(1)}, bf16[128,1024]{1,0:T(8,128)(2,1)}, u32[]{:S(2)}) copy-start(bf16[128,1024]{1,0:T(8,128)(2,1)} %param.32) | copy-start | bytes 786436
  27.6 0.7 copy-start.13
  29.6 19.7 %all-to-all-start.2 = ((f32[8,2,1024]{2,1,0:T(2,128)}), f32[8,2,1024]{2,1,0:T(2,128)S(1)}, u32[]{:S(2)}, u32[]{:S(2)}) async-start(f32[8,2,1024]{2,1,0:T(2,128)} %broadcast_in_dim.107), calls=%async_computation.2 | async-start | bytes 131072 | tf_op jit(solution)/shard_map/all_to_all | solution.py:20
  34.4 39.6 %collective-permute-start.1 = (bf16[1026,128]{1,0:T(8,128)(2,1)S(1)}, bf16[1026,128]{1,0:T(8,128)(2,1)S(1)}, u32[]{:S(2)}, u32[]{:S(2)}) collective-permute-start(bf16[1026,128]{1,0:T(8,128)(2,1)S(1)} %concatenate.7), channel_id=1, source_target_pairs={{256,0},{264,8},{272,16},{280,24},{288,32},{296,40},{304,48},{312,... | collective-permute-start | bytes 787976 | tf_op jit(solution)/shard_map/ppermute | solution.py:12
  49.3 0.7 copy-start.14
  50.0 23.3 %collective-permute-start = (bf16[1,1024]{1,0:T(2,128)(2,1)S(1)}, bf16[1,1024]{1,0:T(2,128)(2,1)S(1)}, u32[]{:S(2)}, u32[]{:S(2)}) collective-permute-start(bf16[1,1024]{1,0:T(2,128)(2,1)S(1)} %constant_dynamic-slice_fusion.2), channel_id=1, source_target_pairs={{256,0},{264,8},{272,16},{280,24},{288,32},{296,40},{304,48},{312,... | collective-permute-start | bytes 6152 | tf_op jit(solution)/shard_map/ppermute | solution.py:12
